TPU v7x, 128 devices: a whole 4x4x4 slice. The times are simulated.
128 devices in a mesh: expert: 64 (over x, y, z), replica: 2 (over core).
Axes of the slice: x: 4, y: 4, z: 4, core: 2. Of those that a mesh axis runs over, the one named last changes fastest.
Arguments:
- x_quant: bfloat16 [16384, 2048], P(('expert', 'replica')), may hold values from -6 to 6
- x_scale: float32 [16384, 16], P(('expert', 'replica')), may hold values from 0.3 to 3
- out_grad: bfloat16 [16384, 2048], P(('expert', 'replica')), may hold values from -6 to 6
- expert_ids: int32 [16384, 8], P(('expert', 'replica')), may hold values from 0 to 63, all different within a row; in each aligned block of 128 rows (0 to 127, 128 to 255, ...) at most 20 rows name the same one
- gate_fixed: int32 [16384, 8], P(('expert', 'replica')), may hold values from 1024 to 16383
- w_gate: bfloat16 [64, 2048, 768], P('expert'), may hold values from -0.125 to 0.125
- s_gate: float32 [64, 16, 6], P('expert'), may hold values from 0.3 to 3
- w_up: bfloat16 [64, 2048, 768], P('expert'), may hold values from -0.125 to 0.125
- s_up: float32 [64, 16, 6], P('expert'), may hold values from 0.3 to 3
- w_down: bfloat16 [64, 768, 2048], P('expert'), may hold values from -0.21875 to 0.21875
- s_down: float32 [64, 6, 16], P('expert'), may hold values from 0.3 to 3
Outputs:
- grad_input: bfloat16 [16384, 2048], P(('expert', 'replica'))
- grad_gate: bfloat16 [64, 2048, 768], P('expert', None, 'replica')
- grad_up: bfloat16 [64, 2048, 768], P('expert', None, 'replica')
- grad_down: bfloat16 [64, 768, 2048], P('expert', 'replica')
Inputs may be any that keep to these rules, and one draw needn't show every extreme that they name: `expert_ids`: each row names 8 different experts. Among the rows of one device at most 20 name the same expert, and in every draw some expert is named by exactly 20 rows of some device.
All inputs are finite; a program needn't handle non-finite values.
Results may differ from a plain program's by a relative error of at most 0.012.
Values may be sent and summed in bfloat16 or wider, within the bound.
No kernel may reach another device: no remote copies, remote signals or barrier semaphores. Data moves between devices by JAX's collectives and lax.ppermute only.
A program may use at most 192 MiB of HBM per device.

v0:
```python
import jax
import jax.numpy as jnp
from jax import lax
from jax.sharding import PartitionSpec as P


def dequant(weight, scale):
    rows, cols = weight.shape
    srows, scols = scale.shape
    blocks = weight.reshape(srows, rows // srows, scols, cols // scols).astype(jnp.float32)
    return (blocks * scale[:, None, :, None]).reshape(rows, cols).astype(jnp.bfloat16)


def forward_parts(xrows, gate_w, up_w):
    pre_gate = jnp.dot(xrows, gate_w, preferred_element_type=jnp.float32)
    pre_up = jnp.dot(xrows, up_w, preferred_element_type=jnp.float32)
    sig = jax.nn.sigmoid(pre_gate)
    act = pre_gate * sig
    return (pre_gate, pre_up, sig, act)


def unit_grads(row_grad, down_w, pre_gate, pre_up, sig, act):
    hidden_grad = jnp.dot(row_grad, down_w.T, preferred_element_type=jnp.float32)
    up_grad = (hidden_grad * act).astype(jnp.bfloat16)
    gate_grad = (hidden_grad * pre_up * sig * (1.0 + pre_gate * (1.0 - sig))).astype(jnp.bfloat16)
    return (gate_grad, up_grad)


def shards(
    x_quant, x_scale, out_grad, expert_ids, gate_fixed, w_gate, s_gate, w_up, s_up, w_down, s_down
):
    tok_rows, width = x_quant.shape
    topk = expert_ids.shape[1]
    experts = lax.axis_size("expert")
    capacity = tok_rows * topk * 5 // (4 * experts)
    blk_width = width // x_scale.shape[1]
    flat_ids = expert_ids.reshape(-1)
    onehot = (flat_ids[:, None] == jnp.arange(experts, dtype=jnp.int32)[None, :]).astype(jnp.int32)
    before = jnp.cumsum(onehot, axis=0) - onehot
    slot_of = jnp.sum(before * onehot, axis=1)
    token_of = jnp.arange(tok_rows * topk, dtype=jnp.int32) // topk
    table = jnp.full((experts, capacity), tok_rows, jnp.int32).at[flat_ids, slot_of].set(token_of)
    gate_vals = gate_fixed.reshape(-1).astype(jnp.float32) / 65536.0
    gate_table = jnp.zeros((experts, capacity), jnp.float32).at[flat_ids, slot_of].set(gate_vals)
    scaled = x_quant.reshape(tok_rows, -1, blk_width).astype(jnp.float32) * x_scale[:, :, None]
    inputs = scaled.reshape(tok_rows, width).astype(jnp.bfloat16)
    input_pad = jnp.concatenate([inputs, jnp.zeros((1, width), jnp.bfloat16)], axis=0)
    grad_pad = jnp.concatenate([out_grad, jnp.zeros((1, width), jnp.bfloat16)], axis=0)
    send_rows = input_pad[table]
    send_grads = (gate_table[:, :, None] * grad_pad[table].astype(jnp.float32)).astype(jnp.bfloat16)
    got_rows, got_grads = (
        lax.all_to_all(send_rows, "expert", split_axis=0, concat_axis=0, tiled=True),
        lax.all_to_all(send_grads, "expert", split_axis=0, concat_axis=0, tiled=True),
    )
    xrows = got_rows.reshape(experts * capacity, width)
    row_grad = got_grads.reshape(experts * capacity, width)
    gate_w = dequant(w_gate[0], s_gate[0])
    up_w = dequant(w_up[0], s_up[0])
    down_w = dequant(w_down[0], s_down[0])
    pre_gate, pre_up, sig, act = forward_parts(xrows, gate_w, up_w)
    hidden = (act * pre_up).astype(jnp.bfloat16)
    gate_grad, up_grad = unit_grads(row_grad, down_w, pre_gate, pre_up, sig, act)
    row_input = jnp.dot(gate_grad, gate_w.T, preferred_element_type=jnp.float32)
    row_input = row_input + jnp.dot(up_grad, up_w.T, preferred_element_type=jnp.float32)
    term_gate = jnp.dot(xrows.T, gate_grad, preferred_element_type=jnp.float32)
    term_up = jnp.dot(xrows.T, up_grad, preferred_element_type=jnp.float32)
    term_down = jnp.dot(hidden.T, row_grad, preferred_element_type=jnp.float32)
    sum_gate, sum_up, sum_down = (
        lax.psum_scatter(
            term_gate.astype(jnp.bfloat16), "replica", scatter_dimension=1, tiled=True
        ).astype(jnp.float32),
        lax.psum_scatter(
            term_up.astype(jnp.bfloat16), "replica", scatter_dimension=1, tiled=True
        ).astype(jnp.float32),
        lax.psum_scatter(
            term_down.astype(jnp.bfloat16), "replica", scatter_dimension=0, tiled=True
        ).astype(jnp.float32),
    )
    back_rows = row_input.astype(jnp.bfloat16).reshape(experts, capacity, width)
    returned = lax.all_to_all(back_rows, "expert", split_axis=0, concat_axis=0, tiled=True)
    picked = returned[expert_ids, slot_of.reshape(tok_rows, topk)].astype(jnp.float32)
    grad_input = jnp.sum(picked, axis=1).astype(jnp.bfloat16)
    grad_gate = sum_gate.astype(jnp.bfloat16)[None]
    grad_up = sum_up.astype(jnp.bfloat16)[None]
    grad_down = sum_down.astype(jnp.bfloat16)[None]
    return (grad_input, grad_gate, grad_up, grad_down)


def solution(mesh):
    placed = (
        P(("expert", "replica"), None),
        P(("expert", "replica"), None),
        P(("expert", "replica"), None),
        P(("expert", "replica"), None),
        P(("expert", "replica"), None),
        P("expert", None, None),
        P("expert", None, None),
        P("expert", None, None),
        P("expert", None, None),
        P("expert", None, None),
        P("expert", None, None),
    )
    return jax.shard_map(
        shards,
        mesh=mesh,
        in_specs=placed,
        out_specs=(
            P(("expert", "replica"), None),
            P("expert", None, "replica"),
            P("expert", None, "replica"),
            P("expert", "replica", None),
        ),
        check_vma=False,
    )
```

profile of v0, /device:TPU:82, one launch (start us, length us, event | category | flops | bytes accessed | tf_op | source)
XLA Modules:
  0.0 488.2 jit_solution(6782455465866707141)
XLA Ops:
  8.3 18.0 %reduce-window.6 = s32[64,8,128]{2,1,0:T(8,128)S(1)} reduce-window(s32[64,8,128]{2,1,0:T(8,128)S(1)} %fusion.23, s32[]{:T(128)} %constant.16.clone.1), window={size=1x1x128 pad=0_0x0_0x127_0}, to_apply=%region_0.0 | reduce-window | flops 8323072 | bytes 524292 | tf_op jit(solution)/shard_map/reduce-window
  41.5 8.9 %reshape.210 = bf16[64,20,2048]{2,1,0:T(8,128)(2,1)} reshape(bf16[1280,2048]{1,0:T(8,128)(2,1)} %gather_fusion.1) | data formatting | bytes 10485760 | tf_op jit(solution)/shard_map/gather | solution.py:49
  50.4 10.7 %all-to-all-start.1 = ((bf16[64,20,2048]{2,1,0:T(8,128)(2,1)}), bf16[64,20,2048]{2,1,0:T(8,128)(2,1)}, u32[]{:S(2)}, u32[]{:S(2)}) async-start(bf16[64,20,2048]{2,1,0:T(8,128)(2,1)} %reshape.210), calls=%async_computation.1 | async-start | bytes 12582912 | tf_op jit(solution)/shard_map/all_to_all | solution.py:52
  61.2 6.2 %gather_fusion = bf16[1280,2048]{1,0:T(8,128)(2,1)} fusion(bf16[129,2048]{1,0:T(8,128)(2,1)S(1)} %concatenate.14, s32[2048]{0:T(1024)S(1)} %pad_clamp_fusion), kind=kCustom, calls=%fused_computation | custom fusion | bytes 10490880 | tf_op jit(solution)/shard_map/gather | solution.py:50
  67.3 9.7 %reshape.239 = f32[64,20,2048]{2,1,0:T(8,128)} reshape(bf16[1280,2048]{1,0:T(8,128)(2,1)} %gather_fusion) | data formatting | bytes 15728640 | tf_op jit(solution)/shard_map/convert_element_type | solution.py:50
  81.7 7.9 %multiply_convert_fusion = bf16[64,20,2048]{2,1,0:T(8,128)(2,1)} fusion(f32[64,20,2048]{2,1,0:T(8,128)} %reshape.239, f32[64,20]{1,0:T(8,128)S(1)} %copy.75), kind=kLoop, calls=%fused_computation.5 | loop fusion | flops 5242880 | bytes 15733760 | tf_op jit(solution)/shard_map/convert_element_type | solution.py:50
  89.6 60.6 %all-to-all-done.1 = bf16[64,20,2048]{2,1,0:T(8,128)(2,1)} async-done(((bf16[64,20,2048]{2,1,0:T(8,128)(2,1)}), bf16[64,20,2048]{2,1,0:T(8,128)(2,1)}, u32[]{:S(2)}, u32[]{:S(2)}) %all-to-all-start.1) | async-done | bytes 5242912 | tf_op jit(solution)/shard_map/all_to_all | solution.py:52
  150.2 10.0 %all-to-all-start = ((bf16[64,20,2048]{2,1,0:T(8,128)(2,1)}), bf16[64,20,2048]{2,1,0:T(8,128)(2,1)}, u32[]{:S(2)}, u32[]{:S(2)}) async-start(bf16[64,20,2048]{2,1,0:T(8,128)(2,1)} %multiply_convert_fusion), calls=%async_computation | async-start | bytes 12582912 | tf_op jit(solution)/shard_map/all_to_all | solution.py:53
  187.7 9.2 %reshape.185 = bf16[1280,2048]{1,0:T(8,128)(2,1)} reshape(bf16[64,20,2048]{2,1,0:T(8,128)(2,1)} %all-to-all-done.1) | data formatting | bytes 10485760 | tf_op jit(solution)/shard_map/reshape | solution.py:55
  196.9 9.8 %fusion.12 = f32[1280,768]{1,0:T(8,128)} fusion(bf16[1280,2048]{1,0:T(8,128)(2,1)} %reshape.185, bf16[96,8,16,128]{3,2,1,0:T(8,128)(2,1)} %bitcast.146), kind=kOutput, calls=%fused_computation.33 | convolution fusion | flops 4026531840 | bytes 12320768 | tf_op jit(solution)/shard_map/dot_general | solution.py:16
  206.7 6.2 %fusion.9 = f32[1280,768]{1,0:T(8,128)} fusion(bf16[1280,2048]{1,0:T(8,128)(2,1)S(1)} %copy-done.1, bf16[96,8,16,128]{3,2,1,0:T(8,128)(2,1)S(1)} %bitcast.147), kind=kOutput, calls=%fused_computation.30 | convolution fusion | flops 4026531840 | bytes 12320768 | tf_op jit(solution)/shard_map/dot_general | solution.py:15
  213.0 37.7 %all-to-all-done = bf16[64,20,2048]{2,1,0:T(8,128)(2,1)} async-done(((bf16[64,20,2048]{2,1,0:T(8,128)(2,1)}), bf16[64,20,2048]{2,1,0:T(8,128)(2,1)}, u32[]{:S(2)}, u32[]{:S(2)}) %all-to-all-start) | async-done | bytes 5242912 | tf_op jit(solution)/shard_map/all_to_all | solution.py:53
  250.7 9.0 %reshape.184 = bf16[1280,2048]{1,0:T(8,128)(2,1)} reshape(bf16[64,20,2048]{2,1,0:T(8,128)(2,1)} %all-to-all-done) | data formatting | bytes 10485760 | tf_op jit(solution)/shard_map/reshape | solution.py:56
  259.7 12.5 %multiply_convert_fusion.4 = (bf16[1280,768]{1,0:T(8,128)(2,1)S(1)}, bf16[1280,768]{1,0:T(8,128)(2,1)}) fusion(f32[1280,768]{1,0:T(8,128)} %fusion.9, f32[1280,768]{1,0:T(8,128)} %fusion.12, bf16[1280,2048]{1,0:T(8,128)(2,1)} %reshape.184, bf16[96,8,16,128]{3,2,1,0:T(8,128)(2,1)} %bitcast.145), kind=kOutput, calls=%fused_computation.22 | convolution fusion | flops 4039311360 | bytes 20185088 | tf_op jit(solution)/shard_map/dot_general | solution.py:23
  273.4 8.8 %convolution_convert_fusion.1 = bf16[2048,768]{1,0:T(8,128)(2,1)} fusion(bf16[1280,2048]{1,0:T(8,128)(2,1)} %reshape.185, bf16[1280,768]{1,0:T(8,128)(2,1)S(1)} %get-tuple-element.4), kind=kOutput, calls=%fused_computation.27 | convolution fusion | flops 4028104704 | bytes 10354688 | tf_op jit(solution)/shard_map/dot_general | solution.py:66
  287.1 9.4 %convolution_convert_fusion.2 = bf16[2048,768]{1,0:T(8,128)(2,1)} fusion(bf16[1280,2048]{1,0:T(8,128)(2,1)} %reshape.185, bf16[1280,768]{1,0:T(8,128)(2,1)} %get-tuple-element.5), kind=kOutput, calls=%fused_computation.28 | convolution fusion | flops 4028104704 | bytes 10354688 | tf_op jit(solution)/shard_map/dot_general | solution.py:65
  303.3 10.3 %fusion.6 = f32[1280,2048]{1,0:T(8,128)} fusion(bf16[1280,768]{1,0:T(8,128)(2,1)} %get-tuple-element.5, bf16[1,2048,768]{1,2,0:T(8,128)(2,1)S(1)} %copy-done, f32[96,8,16,128]{3,2,1,0:T(8,128)S(1)} %bitcast.141), kind=kOutput, calls=%fused_computation.29 | convolution fusion | flops 4031250432 | bytes 21889024 | tf_op jit(solution)/shard_map/dot_general | solution.py:63
  313.6 6.1 %convolution_convert_fusion = bf16[768,2048]{1,0:T(8,128)(2,1)} fusion(bf16[1280,2048]{1,0:T(8,128)(2,1)S(1)} %bitcast.143, f32[1280,768]{1,0:T(8,128)S(1)} %copy-done.15, f32[1280,768]{1,0:T(8,128)S(1)} %copy-done.16), kind=kOutput, calls=%fused_computation.26 | convolution fusion | flops 4034002944 | bytes 16252928 | tf_op jit(solution)/shard_map/dot_general | solution.py:67
  321.4 10.3 %add_convert_fusion = bf16[1280,2048]{1,0:T(8,128)(2,1)} fusion(f32[1280,2048]{1,0:T(8,128)} %fusion.6, bf16[1280,768]{1,0:T(8,128)(2,1)S(1)} %copy-done.14, bf16[1,2048,768]{1,2,0:T(8,128)(2,1)S(1)} %copy.78, f32[96,8,16,128]{3,2,1,0:T(8,128)S(1)} %bitcast.140), kind=kOutput, calls=%fused_computation.6 | convolution fusion | flops 4036493312 | bytes 27131904 | tf_op jit(solution)/shard_map/dot_general | solution.py:64
  331.6 9.1 %reshape.186 = bf16[64,20,2048]{2,1,0:T(8,128)(2,1)} reshape(bf16[1280,2048]{1,0:T(8,128)(2,1)} %add_convert_fusion) | data formatting | bytes 10485760 | tf_op jit(solution)/shard_map/reshape | solution.py:79
  340.7 9.4 %all-to-all-start.2 = ((bf16[64,20,2048]{2,1,0:T(8,128)(2,1)}), bf16[64,20,2048]{2,1,0:T(8,128)(2,1)}, u32[]{:S(2)}, u32[]{:S(2)}) async-start(bf16[64,20,2048]{2,1,0:T(8,128)(2,1)} %reshape.186), calls=%async_computation.2 | async-start | bytes 12582912 | tf_op jit(solution)/shard_map/all_to_all | solution.py:80
  350.5 86.5 %all-to-all-done.2 = bf16[64,20,2048]{2,1,0:T(8,128)(2,1)} async-done(((bf16[64,20,2048]{2,1,0:T(8,128)(2,1)}), bf16[64,20,2048]{2,1,0:T(8,128)(2,1)}, u32[]{:S(2)}, u32[]{:S(2)}) %all-to-all-start.2) | async-done | bytes 5242912 | tf_op jit(solution)/shard_map/all_to_all | solution.py:80
  437.1 8.0 %copy.84 = bf16[64,20,2048]{2,0,1:T(8,128)(2,1)} copy(bf16[64,20,2048]{2,1,0:T(8,128)(2,1)} %all-to-all-done.2) | data formatting | bytes 10485760 | tf_op jit(solution)/shard_map/all_to_all | solution.py:80
  445.1 25.3 %gather_fusion.2 = bf16[1024,2048]{1,0:T(8,128)(2,1)} fusion(bf16[64,20,2048]{2,0,1:T(8,128)(2,1)} %copy.84, s32[1024]{0:T(1024)S(1)} %reshape.217), kind=kCustom, calls=%fused_computation.2 | custom fusion | bytes 8396800 | tf_op jit(solution)/shard_map/gather | solution.py:81
  (114 shorter events, 74.1 us)
Async XLA Ops:
  7.2 27.7 %copy-start.5 = (bf16[128,2048]{1,0:T(8,128)(2,1)S(1)}, bf16[128,2048]{1,0:T(8,128)(2,1)}, u32[]{:S(2)}) copy-start(bf16[128,2048]{1,0:T(8,128)(2,1)} %param.11) | copy-start | bytes 1572868
  50.4 10.7 %copy-start.4 = (bf16[128,2048]{1,0:T(8,128)(2,1)S(1)}, bf16[128,2048]{1,0:T(8,128)(2,1)}, u32[]{:S(2)}) copy-start(bf16[128,2048]{1,0:T(8,128)(2,1)} %param.13) | copy-start | bytes 1572868
  50.4 99.8 %all-to-all-start.1 = ((bf16[64,20,2048]{2,1,0:T(8,128)(2,1)}), bf16[64,20,2048]{2,1,0:T(8,128)(2,1)}, u32[]{:S(2)}, u32[]{:S(2)}) async-start(bf16[64,20,2048]{2,1,0:T(8,128)(2,1)} %reshape.210), calls=%async_computation.1 | async-start | bytes 12582912 | tf_op jit(solution)/shard_map/all_to_all | solution.py:52
  67.3 9.7 %copy-start.9 = (s32[128,8]{0,1:T(8,128)S(1)}, s32[128,8]{0,1:T(8,128)}, u32[]{:S(2)}) copy-start(s32[128,8]{0,1:T(8,128)} %param.15) | copy-start | bytes 12292
  150.2 100.5 %all-to-all-start = ((bf16[64,20,2048]{2,1,0:T(8,128)(2,1)}), bf16[64,20,2048]{2,1,0:T(8,128)(2,1)}, u32[]{:S(2)}, u32[]{:S(2)}) async-start(bf16[64,20,2048]{2,1,0:T(8,128)(2,1)} %multiply_convert_fusion), calls=%async_computation | async-start | bytes 12582912 | tf_op jit(solution)/shard_map/all_to_all | solution.py:53
  160.2 316.1 %reduce-scatter.12.cloned.1.call-start = ((), (), s32[]{:S(2)}) async-start(), calls=%async_computation.8 | async-start | bytes 4718592
  164.5 4.1 copy-start.10
  176.0 1.9 copy-start.2
  177.9 2.4 slice-start
  178.8 1.5 copy-start.12
  178.8 2.2 slice-start.1
  196.9 9.9 %copy-start.1 = (bf16[1280,2048]{1,0:T(8,128)(2,1)S(1)}, bf16[1280,2048]{1,0:T(8,128)(2,1)}, u32[]{:S(2)}) copy-start(bf16[1280,2048]{1,0:T(8,128)(2,1)} %reshape.185) | copy-start | bytes 15728644
  196.9 9.8 %copy-start.3 = (bf16[16,128,6,128]{1,0,3,2:T(8,128)(2,1)S(1)}, bf16[16,128,6,128]{1,0,3,2:T(8,128)(2,1)}, u32[]{:S(2)}) copy-start(bf16[16,128,6,128]{1,0,3,2:T(8,128)(2,1)} %multiply_convert_fusion.1) | copy-start | bytes 9437188
  287.0 191.9 %reduce-scatter.10.cloned.1.call-start = ((), (), s32[]{:S(2)}) async-start(), calls=%async_computation.7 | async-start | bytes 4718592
  301.4 180.1 %reduce-scatter.8.cloned.1.call-start = ((), (), s32[]{:S(2)}) async-start(), calls=%async_computation.6 | async-start | bytes 4718592 | tf_op jit(solution)/shard_map/reduce_scatter | solution.py:75
  301.4 1.9 copy-start
  301.4 12.2 %slice-start.2 = ((s8[5242880]{0:T(1024)(128)(4,1)}), s8[4194304]{0:T(1024)(128)(4,1)S(1)}, s32[]{:S(2)}) async-start(s8[5242880]{0:T(1024)(128)(4,1)} %bitcast.142), calls=%async_computation.11 | async-start | bytes 8388608
  303.3 10.3 %slice-start.3 = ((s8[5242880]{0:T(1024)(128)(4,1)}), s8[1048576]{0:T(1024)(128)(4,1)S(1)}, s32[]{:S(2)}) async-start(s8[5242880]{0:T(1024)(128)(4,1)} %bitcast.142), calls=%async_computation.12 | async-start | bytes 2097152
  303.3 10.3 %copy-start.15 = (f32[1280,768]{1,0:T(8,128)S(1)}, f32[1280,768]{1,0:T(8,128)}, u32[]{:S(2)}) copy-start(f32[1280,768]{1,0:T(8,128)} %fusion.12) | copy-start | bytes 11796484
  303.3 10.3 %copy-start.16 = (f32[1280,768]{1,0:T(8,128)S(1)}, f32[1280,768]{1,0:T(8,128)}, u32[]{:S(2)}) copy-start(f32[1280,768]{1,0:T(8,128)} %fusion.9) | copy-start | bytes 11796484
  319.8 1.5 copy-start.14
  340.7 9.4 %copy-start.7 = (s32[1024]{0:T(1024)S(1)}, s32[1024]{0:T(1024)}, u32[]{:S(2)}) copy-start(s32[1024]{0:T(1024)} %copy-done.6) | copy-start | bytes 12292
  340.7 9.6 %copy-start.8 = (s32[128,8]{0,1:T(8,128)S(1)}, s32[128,8]{0,1:T(8,128)}, u32[]{:S(2)}) copy-start(s32[128,8]{0,1:T(8,128)} %param.14) | copy-start | bytes 12292
  340.7 96.3 %all-to-all-start.2 = ((bf16[64,20,2048]{2,1,0:T(8,128)(2,1)}), bf16[64,20,2048]{2,1,0:T(8,128)(2,1)}, u32[]{:S(2)}, u32[]{:S(2)}) async-start(bf16[64,20,2048]{2,1,0:T(8,128)(2,1)} %reshape.186), calls=%async_computation.2 | async-start | bytes 12582912 | tf_op jit(solution)/shard_map/all_to_all | solution.py:80
  (3 other events, 3.4 us)
Sparse Core Ops, SparseCore 0:
  287.1 13.4 reduce-scatter.11
  303.0 14.9 reduce-scatter.9
  320.9 14.9 reduce-scatter.7
where the time goes:
time: 497 us; the launch traced here: 488 us
  waiting for transfers between devices  185 us (37%)
  local copies, waits for them, and re-layouts  140 us (28%)
  matrix products  73.4 us (15%)
  other arithmetic  45.1 us (9%)
  starting transfers between devices  30.4 us (6%)
  between operations  14.4 us (3%)
    all_to_all x1, waiting for transfers between devices, shards(): lax.all_to_all(back_rows, 'expert', split_axis=0, concat_axis=0, tiled=True)  86.5 us
    all_to_all x1, waiting for transfers between devices, shards(): lax.all_to_all(send_rows, 'expert', split_axis=0, concat_axis=0, tiled=True)  60.6 us
    unnamed x60, local copies, waits for them, and re-layouts  45.6 us
    all_to_all x1, waiting for transfers between devices, shards(): lax.all_to_all(send_grads, 'expert', split_axis=0, concat_axis=0, tiled=T...  37.7 us
    gather x1, local copies, waits for them, and re-layouts, shards(): returned[expert_ids, slot_of.reshape(tok_rows, topk)].astype(jnp.float32)  25.3 us
    another operation x3, other arithmetic  18.2 us
    gather x2, local copies, waits for them, and re-layouts, shards(): send_rows = input_pad[table]  15 us
    dot_general x1, matrix products, unit_grads(): jnp.dot(row_grad, down_w.T, preferred_element_type=jnp.float32)  12.5 us
  transfers between devices with their start and end apart: 6, of which 3 were waited for; matrix products, arithmetic and copies ran while one was open for 36% of the time, Pallas kernels for 0%

commit v1 on v0

--- a/solution.py
+++ b/solution.py
@@ -2,6 +2,8 @@
 import jax.numpy as jnp
 from jax import lax
 from jax.sharding import PartitionSpec as P
+
+LANES = 128
 
 
 def dequant(weight, scale):
@@ -26,6 +28,30 @@
     return (gate_grad, up_grad)
 
 
+def routing(expert_ids, gate_fixed, experts, capacity):
+    tok_rows, topk = expert_ids.shape
+    n = tok_rows * topk
+    flat_ids = expert_ids.reshape(-1)
+    onehot = flat_ids[:, None] == jnp.arange(experts, dtype=jnp.int32)[None, :]
+    order = jnp.arange(n, dtype=jnp.int32)
+    lower = (order[None, :] < order[:, None]).astype(jnp.bfloat16)
+    before = jnp.dot(lower, onehot.astype(jnp.bfloat16), preferred_element_type=jnp.float32)
+    slot_of = jnp.sum(jnp.where(onehot, before, 0.0), axis=1).astype(jnp.int32)
+    dest = flat_ids * capacity + slot_of
+    places = jnp.arange(experts * capacity, dtype=jnp.int32)
+    pick = (dest[None, :] == places[:, None]).astype(jnp.bfloat16)
+    flat_gate = gate_fixed.reshape(-1)
+    token_of = order // topk
+    cols = jnp.stack(
+        [token_of, jnp.ones_like(token_of), flat_gate // 128, flat_gate % 128], axis=1
+    ).astype(jnp.bfloat16)
+    got = jnp.dot(pick, cols, preferred_element_type=jnp.float32)
+    used = got[:, 1] > 0.5
+    table = jnp.where(used, got[:, 0], float(tok_rows)).astype(jnp.int32)
+    gate_table = (got[:, 2] * 128.0 + got[:, 3]) / 65536.0
+    return dest, table, gate_table
+
+
 def shards(
     x_quant, x_scale, out_grad, expert_ids, gate_fixed, w_gate, s_gate, w_up, s_up, w_down, s_down
 ):
@@ -33,27 +59,27 @@
     topk = expert_ids.shape[1]
     experts = lax.axis_size("expert")
     capacity = tok_rows * topk * 5 // (4 * experts)
+    sub = width // LANES
     blk_width = width // x_scale.shape[1]
-    flat_ids = expert_ids.reshape(-1)
-    onehot = (flat_ids[:, None] == jnp.arange(experts, dtype=jnp.int32)[None, :]).astype(jnp.int32)
-    before = jnp.cumsum(onehot, axis=0) - onehot
-    slot_of = jnp.sum(before * onehot, axis=1)
-    token_of = jnp.arange(tok_rows * topk, dtype=jnp.int32) // topk
-    table = jnp.full((experts, capacity), tok_rows, jnp.int32).at[flat_ids, slot_of].set(token_of)
-    gate_vals = gate_fixed.reshape(-1).astype(jnp.float32) / 65536.0
-    gate_table = jnp.zeros((experts, capacity), jnp.float32).at[flat_ids, slot_of].set(gate_vals)
+    dest, table, gate_table = routing(expert_ids, gate_fixed, experts, capacity)
     scaled = x_quant.reshape(tok_rows, -1, blk_width).astype(jnp.float32) * x_scale[:, :, None]
-    inputs = scaled.reshape(tok_rows, width).astype(jnp.bfloat16)
-    input_pad = jnp.concatenate([inputs, jnp.zeros((1, width), jnp.bfloat16)], axis=0)
-    grad_pad = jnp.concatenate([out_grad, jnp.zeros((1, width), jnp.bfloat16)], axis=0)
+    inputs = scaled.reshape(tok_rows, sub, LANES).astype(jnp.bfloat16)
+    zero_row = jnp.zeros((1, sub, LANES), jnp.bfloat16)
+    input_pad = jnp.concatenate([inputs, zero_row], axis=0)
+    grad_pad = jnp.concatenate([out_grad.reshape(tok_rows, sub, LANES), zero_row], axis=0)
     send_rows = input_pad[table]
-    send_grads = (gate_table[:, :, None] * grad_pad[table].astype(jnp.float32)).astype(jnp.bfloat16)
-    got_rows, got_grads = (
-        lax.all_to_all(send_rows, "expert", split_axis=0, concat_axis=0, tiled=True),
-        lax.all_to_all(send_grads, "expert", split_axis=0, concat_axis=0, tiled=True),
+    send_grads = (gate_table[:, None, None] * grad_pad[table].astype(jnp.float32)).astype(jnp.bfloat16)
+    payload = jnp.concatenate(
+        [
+            send_rows.reshape(experts, capacity * sub, LANES),
+            send_grads.reshape(experts, capacity * sub, LANES),
+        ],
+        axis=1,
     )
-    xrows = got_rows.reshape(experts * capacity, width)
-    row_grad = got_grads.reshape(experts * capacity, width)
+    got = lax.all_to_all(payload, "expert", split_axis=0, concat_axis=0, tiled=True)
+    rows_in = experts * capacity
+    xrows = got[:, : capacity * sub].reshape(rows_in, width)
+    row_grad = got[:, capacity * sub :].reshape(rows_in, width)
     gate_w = dequant(w_gate[0], s_gate[0])
     up_w = dequant(w_up[0], s_up[0])
     down_w = dequant(w_down[0], s_down[0])
@@ -62,6 +88,8 @@
     gate_grad, up_grad = unit_grads(row_grad, down_w, pre_gate, pre_up, sig, act)
     row_input = jnp.dot(gate_grad, gate_w.T, preferred_element_type=jnp.float32)
     row_input = row_input + jnp.dot(up_grad, up_w.T, preferred_element_type=jnp.float32)
+    back_rows = row_input.astype(jnp.bfloat16).reshape(experts, capacity * sub, LANES)
+    returned = lax.all_to_all(back_rows, "expert", split_axis=0, concat_axis=0, tiled=True)
     term_gate = jnp.dot(xrows.T, gate_grad, preferred_element_type=jnp.float32)
     term_up = jnp.dot(xrows.T, up_grad, preferred_element_type=jnp.float32)
     term_down = jnp.dot(hidden.T, row_grad, preferred_element_type=jnp.float32)
@@ -76,10 +104,9 @@
             term_down.astype(jnp.bfloat16), "replica", scatter_dimension=0, tiled=True
         ).astype(jnp.float32),
     )
-    back_rows = row_input.astype(jnp.bfloat16).reshape(experts, capacity, width)
-    returned = lax.all_to_all(back_rows, "expert", split_axis=0, concat_axis=0, tiled=True)
-    picked = returned[expert_ids, slot_of.reshape(tok_rows, topk)].astype(jnp.float32)
-    grad_input = jnp.sum(picked, axis=1).astype(jnp.bfloat16)
+    picked = returned.reshape(rows_in, sub, LANES)[dest].astype(jnp.float32)
+    grad_input = jnp.sum(picked.reshape(tok_rows, topk, sub, LANES), axis=1)
+    grad_input = grad_input.reshape(tok_rows, width).astype(jnp.bfloat16)
     grad_gate = sum_gate.astype(jnp.bfloat16)[None]
     grad_up = sum_up.astype(jnp.bfloat16)[None]
     grad_down = sum_down.astype(jnp.bfloat16)[None]

time: 497 us -> 449 us (0.903)
  local copies, waits for them, and re-layouts: 140 us -> 96.6 us
  waiting for transfers between devices: 185 us -> 211 us
  other arithmetic: 45.1 us -> 26.6 us
  starting transfers between devices: 30.4 us -> 19.9 us
    all_to_all x2 -> x1, waiting for transfers between devices: 98.4 us -> 139 us  [shards(): lax.all_to_all(payload, 'expert', split_axis=0, concat_axis=0, tiled=True)]
    another operation x3 -> x2, other arithmetic: 18.2 us -> 0.05 us
    all_to_all x1, waiting for transfers between devices: 86.5 us -> 71.6 us  [shards(): lax.all_to_all(back_rows, 'expert', split_axis=0, concat_axis=0, tiled=True)]
    gather x1, local copies, waits for them, and re-layouts: 25.3 us -> 10.9 us  [shards(): picked = returned.reshape(rows_in, sub, LANES)[dest].astype(jnp.float32)]
    all_to_all x2 -> x1, starting transfers between devices: 20.7 us -> 10.6 us  [shards(): lax.all_to_all(payload, 'expert', split_axis=0, concat_axis=0, tiled=True)]
    gather x2 -> x1, local copies, waits for them, and re-layouts: 15 us -> 5.09 us  [shards(): send_rows = input_pad[table]]
    convert_element_type x1 -> x0, local copies, waits for them, and re-layouts: 9.67 us -> none  [shards(): grad_pad[table].astype(jnp.float32)]
    slice x2 -> x1, local copies, waits for them, and re-layouts: 0.26 us -> 8.7 us  [shards(): row_grad = got[:, capacity * sub:].reshape(rows_in, width)]
  transfers between devices with their start and end apart: 6 -> 5, of which waited for: 3 -> 2; matrix products, arithmetic and copies ran while one was open for 36% -> 21% of each run, Pallas kernels for 0% -> 0%
where the time goes in v1:
time: 449 us; the launch traced here: 443 us
  waiting for transfers between devices  211 us (47%)
  local copies, waits for them, and re-layouts  96.6 us (22%)
  matrix products  75 us (17%)
  other arithmetic  26.6 us (6%)
  starting transfers between devices  19.9 us (4%)
  between operations  14.4 us (3%)
    all_to_all x1, waiting for transfers between devices, shards(): lax.all_to_all(payload, 'expert', split_axis=0, concat_axis=0, tiled=True)  139 us
    all_to_all x1, waiting for transfers between devices, shards(): lax.all_to_all(back_rows, 'expert', split_axis=0, concat_axis=0, tiled=True)  71.6 us
    unnamed x62, local copies, waits for them, and re-layouts  38 us
    dot_general x1, matrix products, unit_grads(): jnp.dot(row_grad, down_w.T, preferred_element_type=jnp.float32)  12.4 us
    gather x1, local copies, waits for them, and re-layouts, shards(): picked = returned.reshape(rows_in, sub, LANES)[dest].astype(jnp.float32)  10.9 us
    all_to_all x1, starting transfers between devices, shards(): lax.all_to_all(payload, 'expert', split_axis=0, concat_axis=0, tiled=True)  10.6 us
    dot_general x1, matrix products, shards(): row_input = jnp.dot(gate_grad, gate_w.T, preferred_element_type=jnp.float32)  10.3 us
    dot_general x1, matrix products, shards(): jnp.dot(up_grad, up_w.T, preferred_element_type=jnp.float32)  10.3 us
  transfers between devices with their start and end apart: 5, of which 2 were waited for; matrix products, arithmetic and copies ran while one was open for 21% of the time, Pallas kernels for 0%

profile of v1, /device:TPU:82, one launch (start us, length us, event | category | flops | bytes accessed | tf_op | source)
XLA Modules:
  0.0 443.1 jit_solution(16889076962480115608)
XLA Ops:
  13.3 5.0 %gather_fusion.1 = bf16[1280,16,128]{2,1,0:T(8,128)(2,1)} fusion(bf16[129,16,128]{2,1,0:T(8,128)(2,1)S(1)} %concatenate.10, s32[2048]{0:T(1024)S(1)} %pad_clamp_fusion), kind=kCustom, calls=%fused_computation.1 | custom fusion | bytes 10490880 | tf_op jit(solution)/shard_map/gather | solution.py:71
  18.3 5.1 %gather_fusion = bf16[1280,16,128]{2,1,0:T(8,128)(2,1)} fusion(bf16[129,16,128]{2,1,0:T(8,128)(2,1)S(1)} %concatenate.9, s32[2048]{0:T(1024)S(1)} %pad_clamp_fusion), kind=kCustom, calls=%fused_computation | custom fusion | bytes 10490880 | tf_op jit(solution)/shard_map/gather | solution.py:70
  23.4 5.9 %fusion = bf16[64,320,128]{2,1,0:T(8,128)(2,1)S(1)} fusion(f32[64,320]{1,0:T(8,128)S(1)} %copy.30, bf16[64,320,128]{2,1,0:T(8,128)(2,1)} %bitcast.127), kind=kLoop, calls=%fused_computation.5 | loop fusion | flops 7864320 | bytes 10567680 | tf_op jit(solution)/shard_map/convert_element_type | solution.py:71
  29.3 7.4 %pad_maximum_fusion = bf16[64,640,128]{2,1,0:T(8,128)(2,1)} fusion(bf16[64,320,128]{2,1,0:T(8,128)(2,1)S(1)} %fusion, bf16[64,320,128]{2,1,0:T(8,128)(2,1)S(1)} %bitcast.128), kind=kLoop, calls=%fused_computation.3 | loop fusion | flops 20971520 | bytes 20971520 | tf_op jit(solution)/shard_map/concatenate | solution.py:72
  36.7 10.6 %all-to-all-start = ((bf16[64,640,128]{2,1,0:T(8,128)(2,1)}), bf16[64,640,128]{2,1,0:T(8,128)(2,1)}, u32[]{:S(2)}, u32[]{:S(2)}) async-start(bf16[64,640,128]{2,1,0:T(8,128)(2,1)} %pad_maximum_fusion), calls=%async_computation | async-start | bytes 20971520 | tf_op jit(solution)/shard_map/all_to_all | solution.py:79
  52.5 4.1 copy.47
  72.5 139.0 %all-to-all-done = bf16[64,640,128]{2,1,0:T(8,128)(2,1)} async-done(((bf16[64,640,128]{2,1,0:T(8,128)(2,1)}), bf16[64,640,128]{2,1,0:T(8,128)(2,1)}, u32[]{:S(2)}, u32[]{:S(2)}) %all-to-all-start) | async-done | bytes 10485792 | tf_op jit(solution)/shard_map/all_to_all | solution.py:79
  211.4 8.7 %fusion.43 = (bf16[64,320,128]{2,1,0:T(8,128)(2,1)}, bf16[64,320,128]{2,1,0:T(8,128)(2,1)}) fusion(bf16[64,640,128]{2,1,0:T(8,128)(2,1)} %all-to-all-done), kind=kLoop, calls=%fused_computation.89 | loop fusion | bytes 20971520 | tf_op jit(solution)/shard_map/slice | solution.py:82
  220.1 9.0 %reshape.313 = bf16[1280,2048]{1,0:T(8,128)(2,1)} reshape(bf16[64,320,128]{2,1,0:T(8,128)(2,1)} %get-tuple-element.7) | data formatting | bytes 10485760 | tf_op jit(solution)/shard_map/reshape | solution.py:81
  229.2 9.8 %fusion.12 = f32[1280,768]{1,0:T(8,128)} fusion(bf16[1280,2048]{1,0:T(8,128)(2,1)} %reshape.313, bf16[96,8,16,128]{3,2,1,0:T(8,128)(2,1)} %bitcast.136), kind=kOutput, calls=%fused_computation.34 | convolution fusion | flops 4026531840 | bytes 12320768 | tf_op jit(solution)/shard_map/dot_general | solution.py:17
  239.0 6.2 %fusion.15 = f32[1280,768]{1,0:T(8,128)} fusion(bf16[1280,2048]{1,0:T(8,128)(2,1)S(1)} %copy-done.3, bf16[96,8,16,128]{3,2,1,0:T(8,128)(2,1)S(1)} %bitcast.137), kind=kOutput, calls=%fused_computation.37 | convolution fusion | flops 4026531840 | bytes 12320768 | tf_op jit(solution)/shard_map/dot_general | solution.py:18
  245.2 8.9 %reshape.312 = bf16[1280,2048]{1,0:T(8,128)(2,1)} reshape(bf16[64,320,128]{2,1,0:T(8,128)(2,1)} %get-tuple-element.6) | data formatting | bytes 10485760 | tf_op jit(solution)/shard_map/reshape | solution.py:82
  254.0 12.4 %multiply_convert_fusion.3 = (bf16[1280,768]{1,0:T(8,128)(2,1)S(1)}, bf16[1280,768]{1,0:T(8,128)(2,1)}) fusion(f32[1280,768]{1,0:T(8,128)} %fusion.12, f32[1280,768]{1,0:T(8,128)} %fusion.15, bf16[1280,2048]{1,0:T(8,128)(2,1)} %reshape.312, bf16[96,8,16,128]{3,2,1,0:T(8,128)(2,1)} %bitcast.135), kind=kOutput, calls=%fused_computation.26 | convolution fusion | flops 4039311360 | bytes 20185088 | tf_op jit(solution)/shard_map/dot_general | solution.py:25
  267.7 8.9 %convolution_convert_fusion.1 = bf16[2048,768]{1,0:T(8,128)(2,1)} fusion(bf16[1280,2048]{1,0:T(8,128)(2,1)} %reshape.313, bf16[1280,768]{1,0:T(8,128)(2,1)S(1)} %get-tuple-element.8), kind=kOutput, calls=%fused_computation.31 | convolution fusion | flops 4028104704 | bytes 10354688 | tf_op jit(solution)/shard_map/dot_general | solution.py:94
  276.6 4.7 %copy.36 = bf16[2048,768]{0,1:T(8,128)(2,1)} copy(bf16[2048,768]{1,0:T(8,128)(2,1)} %convolution_convert_fusion.1) | data formatting | bytes 6291456
  281.4 9.4 %convolution_convert_fusion.2 = bf16[2048,768]{1,0:T(8,128)(2,1)} fusion(bf16[1280,2048]{1,0:T(8,128)(2,1)} %reshape.313, bf16[1280,768]{1,0:T(8,128)(2,1)} %get-tuple-element.9), kind=kOutput, calls=%fused_computation.32 | convolution fusion | flops 4028104704 | bytes 10354688 | tf_op jit(solution)/shard_map/dot_general | solution.py:93
  290.8 4.9 %copy.34 = bf16[2048,768]{0,1:T(8,128)(2,1)} copy(bf16[2048,768]{1,0:T(8,128)(2,1)} %convolution_convert_fusion.2) | data formatting | bytes 6291456
  297.7 10.3 %fusion.9 = f32[1280,2048]{1,0:T(8,128)} fusion(bf16[1280,768]{1,0:T(8,128)(2,1)} %get-tuple-element.9, bf16[1,2048,768]{1,2,0:T(8,128)(2,1)S(1)} %copy-done.2, f32[96,8,16,128]{3,2,1,0:T(8,128)S(1)} %bitcast.132), kind=kOutput, calls=%fused_computation.33 | convolution fusion | flops 4031250432 | bytes 21889024 | tf_op jit(solution)/shard_map/dot_general | solution.py:89
  308.0 6.1 %convolution_convert_fusion = bf16[768,2048]{1,0:T(8,128)(2,1)} fusion(bf16[1280,2048]{1,0:T(8,128)(2,1)S(1)} %bitcast.134, f32[1280,768]{1,0:T(8,128)S(1)} %copy-done.17, f32[1280,768]{1,0:T(8,128)S(1)} %copy-done.16), kind=kOutput, calls=%fused_computation.30 | convolution fusion | flops 4034002944 | bytes 16252928 | tf_op jit(solution)/shard_map/dot_general | solution.py:95
  315.7 10.3 %add_convert_fusion = bf16[1280,2048]{1,0:T(8,128)(2,1)} fusion(f32[1280,2048]{1,0:T(8,128)} %fusion.9, bf16[1280,768]{1,0:T(8,128)(2,1)S(1)} %copy-done.15, bf16[1,2048,768]{1,2,0:T(8,128)(2,1)S(1)} %copy.31, f32[96,8,16,128]{3,2,1,0:T(8,128)S(1)} %bitcast.131), kind=kOutput, calls=%fused_computation.6 | convolution fusion | flops 4036493312 | bytes 27131904 | tf_op jit(solution)/shard_map/dot_general | solution.py:90
  326.0 9.2 %reshape.314 = bf16[64,320,128]{2,1,0:T(8,128)(2,1)} reshape(bf16[1280,2048]{1,0:T(8,128)(2,1)} %add_convert_fusion) | data formatting | bytes 10485760 | tf_op jit(solution)/shard_map/reshape | solution.py:91
  335.2 9.0 %all-to-all-start.1 = ((bf16[64,320,128]{2,1,0:T(8,128)(2,1)}), bf16[64,320,128]{2,1,0:T(8,128)(2,1)}, u32[]{:S(2)}, u32[]{:S(2)}) async-start(bf16[64,320,128]{2,1,0:T(8,128)(2,1)} %reshape.314), calls=%async_computation.1 | async-start | bytes 10485760 | tf_op jit(solution)/shard_map/all_to_all | solution.py:92
  344.5 71.6 %all-to-all-done.1 = bf16[64,320,128]{2,1,0:T(8,128)(2,1)} async-done(((bf16[64,320,128]{2,1,0:T(8,128)(2,1)}), bf16[64,320,128]{2,1,0:T(8,128)(2,1)}, u32[]{:S(2)}, u32[]{:S(2)}) %all-to-all-start.1) | async-done | bytes 5242912 | tf_op jit(solution)/shard_map/all_to_all | solution.py:92
  416.1 10.9 %gather_fusion.2 = bf16[1024,16,128]{2,1,0:T(8,128)(2,1)} fusion(bf16[1280,16,128]{2,1,0:T(8,128)(2,1)} %bitcast.5, s32[1024]{0:T(1024)S(1)} %broadcast_clamp_fusion), kind=kCustom, calls=%fused_computation.2 | custom fusion | bytes 8392704 | tf_op jit(solution)/shard_map/gather | solution.py:107
  (104 shorter events, 41.3 us)
Async XLA Ops:
  7.2 5.1 %copy-start.6 = (bf16[128,2048]{1,0:T(8,128)(2,1)S(1)}, bf16[128,2048]{1,0:T(8,128)(2,1)}, u32[]{:S(2)}) copy-start(bf16[128,2048]{1,0:T(8,128)(2,1)} %param.11) | copy-start | bytes 1572868
  8.1 4.5 %copy-start.10 = (f32[128,16]{0,1:T(8,128)S(1)}, f32[128,16]{0,1:T(8,128)}, u32[]{:S(2)}) copy-start(f32[128,16]{0,1:T(8,128)} %param.12) | copy-start | bytes 24580
  8.7 3.4 copy-start.8
  23.4 5.9 %copy-start = (bf16[1280,16,128]{2,1,0:T(8,128)(2,1)S(1)}, bf16[1280,16,128]{2,1,0:T(8,128)(2,1)}, u32[]{:S(2)}) copy-start(bf16[1280,16,128]{2,1,0:T(8,128)(2,1)} %gather_fusion) | copy-start | bytes 15728644
  36.7 174.7 %all-to-all-start = ((bf16[64,640,128]{2,1,0:T(8,128)(2,1)}), bf16[64,640,128]{2,1,0:T(8,128)(2,1)}, u32[]{:S(2)}, u32[]{:S(2)}) async-start(bf16[64,640,128]{2,1,0:T(8,128)(2,1)} %pad_maximum_fusion), calls=%async_computation | async-start | bytes 20971520 | tf_op jit(solution)/shard_map/all_to_all | solution.py:79
  47.3 383.9 %reduce-scatter.12.cloned.1.call-start = ((), (), s32[]{:S(2)}) async-start(), calls=%async_computation.7 | async-start | bytes 4718592
  50.8 1.7 copy-start.1
  52.5 4.1 copy-start.11
  60.6 1.9 copy-start.4
  62.5 2.4 slice-start
  63.4 1.5 copy-start.13
  63.4 2.2 slice-start.1
  229.1 9.8 %copy-start.3 = (bf16[1280,2048]{1,0:T(8,128)(2,1)S(1)}, bf16[1280,2048]{1,0:T(8,128)(2,1)}, u32[]{:S(2)}) copy-start(bf16[1280,2048]{1,0:T(8,128)(2,1)} %reshape.313) | copy-start | bytes 15728644
  229.2 9.8 %copy-start.5 = (bf16[16,128,6,128]{1,0,3,2:T(8,128)(2,1)S(1)}, bf16[16,128,6,128]{1,0,3,2:T(8,128)(2,1)}, u32[]{:S(2)}) copy-start(bf16[16,128,6,128]{1,0,3,2:T(8,128)(2,1)} %multiply_convert_fusion.1) | copy-start | bytes 9437188
  281.4 152.5 %reduce-scatter.10.cloned.1.call-start = ((), (), s32[]{:S(2)}) async-start(), calls=%async_computation.6 | async-start | bytes 4718592
  295.7 140.7 %reduce-scatter.8.cloned.1.call-start = ((), (), s32[]{:S(2)}) async-start(), calls=%async_computation.5 | async-start | bytes 4718592 | tf_op jit(solution)/shard_map/reduce_scatter | solution.py:103
  295.8 1.9 copy-start.2
  295.8 12.2 %slice-start.2 = ((s8[5242880]{0:T(1024)(128)(4,1)}), s8[4194304]{0:T(1024)(128)(4,1)S(1)}, s32[]{:S(2)}) async-start(s8[5242880]{0:T(1024)(128)(4,1)} %bitcast.133), calls=%async_computation.10 | async-start | bytes 8388608
  297.7 10.3 %slice-start.3 = ((s8[5242880]{0:T(1024)(128)(4,1)}), s8[1048576]{0:T(1024)(128)(4,1)S(1)}, s32[]{:S(2)}) async-start(s8[5242880]{0:T(1024)(128)(4,1)} %bitcast.133), calls=%async_computation.11 | async-start | bytes 2097152
  297.7 10.3 %copy-start.16 = (f32[1280,768]{1,0:T(8,128)S(1)}, f32[1280,768]{1,0:T(8,128)}, u32[]{:S(2)}) copy-start(f32[1280,768]{1,0:T(8,128)} %fusion.12) | copy-start | bytes 11796484
  297.7 10.3 %copy-start.17 = (f32[1280,768]{1,0:T(8,128)S(1)}, f32[1280,768]{1,0:T(8,128)}, u32[]{:S(2)}) copy-start(f32[1280,768]{1,0:T(8,128)} %fusion.15) | copy-start | bytes 11796484
  335.2 9.0 %copy-start.9 = (f32[1024]{0:T(1024)S(1)}, f32[1024]{0:T(1024)}, u32[]{:S(2)}) copy-start(f32[1024]{0:T(1024)} %copy-done.8) | copy-start | bytes 12292
  335.2 9.1 %copy-start.7 = (s32[128,8]{0,1:T(8,128)S(1)}, s32[128,8]{0,1:T(8,128)}, u32[]{:S(2)}) copy-start(s32[128,8]{0,1:T(8,128)} %param.14) | copy-start | bytes 12292
  335.2 80.9 %all-to-all-start.1 = ((bf16[64,320,128]{2,1,0:T(8,128)(2,1)}), bf16[64,320,128]{2,1,0:T(8,128)(2,1)}, u32[]{:S(2)}, u32[]{:S(2)}) async-start(bf16[64,320,128]{2,1,0:T(8,128)(2,1)} %reshape.314), calls=%async_computation.1 | async-start | bytes 10485760 | tf_op jit(solution)/shard_map/all_to_all | solution.py:92
  (3 other events, 4.4 us)
Sparse Core Ops, SparseCore 0:
  281.5 13.4 reduce-scatter.11
  297.4 14.9 reduce-scatter.9
  315.3 14.9 reduce-scatter.7

commit v2 on v1

--- a/solution.py
+++ b/solution.py
@@ -4,6 +4,7 @@
 from jax.sharding import PartitionSpec as P
 
 LANES = 128
+CHUNKS = 4
 
 
 def dequant(weight, scale):
@@ -59,6 +60,8 @@
     topk = expert_ids.shape[1]
     experts = lax.axis_size("expert")
     capacity = tok_rows * topk * 5 // (4 * experts)
+    chunks = CHUNKS if capacity % CHUNKS == 0 else 1
+    per = capacity // chunks
     sub = width // LANES
     blk_width = width // x_scale.shape[1]
     dest, table, gate_table = routing(expert_ids, gate_fixed, experts, capacity)
@@ -67,32 +70,56 @@
     zero_row = jnp.zeros((1, sub, LANES), jnp.bfloat16)
     input_pad = jnp.concatenate([inputs, zero_row], axis=0)
     grad_pad = jnp.concatenate([out_grad.reshape(tok_rows, sub, LANES), zero_row], axis=0)
-    send_rows = input_pad[table]
-    send_grads = (gate_table[:, None, None] * grad_pad[table].astype(jnp.float32)).astype(jnp.bfloat16)
-    payload = jnp.concatenate(
-        [
-            send_rows.reshape(experts, capacity * sub, LANES),
-            send_grads.reshape(experts, capacity * sub, LANES),
-        ],
-        axis=1,
-    )
-    got = lax.all_to_all(payload, "expert", split_axis=0, concat_axis=0, tiled=True)
-    rows_in = experts * capacity
-    xrows = got[:, : capacity * sub].reshape(rows_in, width)
-    row_grad = got[:, capacity * sub :].reshape(rows_in, width)
+    table = table.reshape(experts, capacity)
+    gate_table = gate_table.reshape(experts, capacity)
     gate_w = dequant(w_gate[0], s_gate[0])
     up_w = dequant(w_up[0], s_up[0])
     down_w = dequant(w_down[0], s_down[0])
-    pre_gate, pre_up, sig, act = forward_parts(xrows, gate_w, up_w)
-    hidden = (act * pre_up).astype(jnp.bfloat16)
-    gate_grad, up_grad = unit_grads(row_grad, down_w, pre_gate, pre_up, sig, act)
-    row_input = jnp.dot(gate_grad, gate_w.T, preferred_element_type=jnp.float32)
-    row_input = row_input + jnp.dot(up_grad, up_w.T, preferred_element_type=jnp.float32)
-    back_rows = row_input.astype(jnp.bfloat16).reshape(experts, capacity * sub, LANES)
-    returned = lax.all_to_all(back_rows, "expert", split_axis=0, concat_axis=0, tiled=True)
-    term_gate = jnp.dot(xrows.T, gate_grad, preferred_element_type=jnp.float32)
-    term_up = jnp.dot(xrows.T, up_grad, preferred_element_type=jnp.float32)
-    term_down = jnp.dot(hidden.T, row_grad, preferred_element_type=jnp.float32)
+    rows_in = experts * per
+    span = per * sub
+
+    def payload_of(c):
+        idx = table[:, c * per : (c + 1) * per]
+        gates = gate_table[:, c * per : (c + 1) * per]
+        send_rows = input_pad[idx]
+        send_grads = (gates[:, :, None, None] * grad_pad[idx].astype(jnp.float32)).astype(jnp.bfloat16)
+        return [send_rows.reshape(experts, span, LANES), send_grads.reshape(experts, span, LANES)]
+
+    def compute(got):
+        xrows = got[:, :span].reshape(rows_in, width)
+        row_grad = got[:, span : 2 * span].reshape(rows_in, width)
+        pre_gate, pre_up, sig, act = forward_parts(xrows, gate_w, up_w)
+        hidden = (act * pre_up).astype(jnp.bfloat16)
+        gate_grad, up_grad = unit_grads(row_grad, down_w, pre_gate, pre_up, sig, act)
+        row_input = jnp.dot(gate_grad, gate_w.T, preferred_element_type=jnp.float32)
+        row_input = row_input + jnp.dot(up_grad, up_w.T, preferred_element_type=jnp.float32)
+        back_rows = row_input.astype(jnp.bfloat16).reshape(experts, span, LANES)
+        part_gate = jnp.dot(xrows.T, gate_grad, preferred_element_type=jnp.float32)
+        part_up = jnp.dot(xrows.T, up_grad, preferred_element_type=jnp.float32)
+        part_down = jnp.dot(hidden.T, row_grad, preferred_element_type=jnp.float32)
+        return back_rows, (part_gate, part_up, part_down)
+
+    terms = None
+    arrived = [None] * chunks
+    backs = [None] * chunks
+    returned = [None] * chunks
+    for step in range(chunks + 2):
+        pieces = []
+        if step < chunks:
+            pieces += payload_of(step)
+        if step >= 2:
+            pieces.append(backs[step - 2])
+        got = lax.all_to_all(
+            jnp.concatenate(pieces, axis=1), "expert", split_axis=0, concat_axis=0, tiled=True
+        )
+        if step < chunks:
+            arrived[step] = got
+        if step >= 2:
+            returned[step - 2] = got[:, -span:]
+        if 1 <= step <= chunks:
+            backs[step - 1], parts = compute(arrived[step - 1])
+            terms = parts if terms is None else tuple(a + b for a, b in zip(terms, parts))
+    term_gate, term_up, term_down = terms
     sum_gate, sum_up, sum_down = (
         lax.psum_scatter(
             term_gate.astype(jnp.bfloat16), "replica", scatter_dimension=1, tiled=True
@@ -104,7 +131,10 @@
             term_down.astype(jnp.bfloat16), "replica", scatter_dimension=0, tiled=True
         ).astype(jnp.float32),
     )
-    picked = returned.reshape(rows_in, sub, LANES)[dest].astype(jnp.float32)
+    back = jnp.concatenate(
+        [r.reshape(experts, per, sub, LANES) for r in returned], axis=1
+    ).reshape(experts * capacity, sub, LANES)
+    picked = back[dest].astype(jnp.float32)
     grad_input = jnp.sum(picked.reshape(tok_rows, topk, sub, LANES), axis=1)
     grad_input = grad_input.reshape(tok_rows, width).astype(jnp.bfloat16)
     grad_gate = sum_gate.astype(jnp.bfloat16)[None]

time: 449 us -> 429 us (0.955)
  the two profiles are of different devices: /device:TPU:82 before, /device:TPU:0 now
where the time goes in v2:
time: 429 us; the launch traced here: 423 us
  local copies, waits for them, and re-layouts  137 us (32%)
  matrix products  91.6 us (21%)
  waiting for transfers between devices  73.6 us (17%)
  starting transfers between devices  58 us (14%)
  other arithmetic  46.6 us (11%)
  between operations  15.3 us (4%)
    all_to_all x6, waiting for transfers between devices, shards(): lax.all_to_all(jnp.concatenate(pieces, axis=1), 'expert', split_axis=0, c...  73.5 us
    all_to_all x6, starting transfers between devices, shards(): lax.all_to_all(jnp.concatenate(pieces, axis=1), 'expert', split_axis=0, c...  57.2 us
    unnamed x172, local copies, waits for them, and re-layouts  50.5 us
    convert_element_type x5, other arithmetic, dequant(): (blocks * scale[:, None, :, None]).reshape(rows, cols).astype(jnp.bfloat16)  17.1 us
    dot_general x4, matrix products, forward_parts(): pre_gate = jnp.dot(xrows, gate_w, preferred_element_type=jnp.float32)  16.7 us
    dot_general x4, matrix products, compute(): part_gate = jnp.dot(xrows.T, gate_grad, preferred_element_type=jnp.float32)  16.1 us
    dot_general x4, matrix products, compute(): part_down = jnp.dot(hidden.T, row_grad, preferred_element_type=jnp.float32)  13.4 us
    reshape x4, local copies, waits for them, and re-layouts, compute(): row_grad = got[:, span:2 * span].reshape(rows_in, width)  13.4 us
  transfers between devices with their start and end apart: 9, of which 5 were waited for; matrix products, arithmetic and copies ran while one was open for 49% of the time, Pallas kernels for 0%

profile of v2, /device:TPU:0, one launch (start us, length us, event | category | flops | bytes accessed | tf_op | source)
XLA Modules:
  0.0 422.5 jit_solution(113331502537489217)
XLA Ops:
  21.2 12.0 %all-to-all-start.2 = ((bf16[64,160,128]{2,1,0:T(8,128)(2,1)}), bf16[64,160,128]{2,1,0:T(8,128)(2,1)}, u32[]{:S(2)}, u32[]{:S(2)}) async-start(bf16[64,160,128]{2,1,0:T(8,128)(2,1)} %pad_maximum_fusion.4), calls=%async_computation.2 | async-start | bytes 5242880 | tf_op jit(solution)/shard_map/all_to_all | solution.py:112
  57.2 4.2 copy.57
  66.7 5.2 %multiply_convert_fusion = bf16[16,128,6,128]{1,0,3,2:T(8,128)(2,1)} fusion(f32[16,128,6,128]{1,0,3,2:T(8,128)} %bitcast.212, f32[16,6]{0,1:T(8,128)S(1)} %bitcast.253), kind=kLoop, calls=%fused_computation.23 | loop fusion | flops 3145728 | bytes 9437568 | tf_op jit(solution)/shard_map/convert_element_type | solution.py:14
  93.5 10.9 %all-to-all-start = ((bf16[64,160,128]{2,1,0:T(8,128)(2,1)}), bf16[64,160,128]{2,1,0:T(8,128)(2,1)}, u32[]{:S(2)}, u32[]{:S(2)}) async-start(bf16[64,160,128]{2,1,0:T(8,128)(2,1)} %pad_maximum_fusion.3), calls=%async_computation | async-start | bytes 5242880 | tf_op jit(solution)/shard_map/all_to_all | solution.py:112
  133.8 5.0 %all-to-all-done = bf16[64,160,128]{2,1,0:T(8,128)(2,1)} async-done(((bf16[64,160,128]{2,1,0:T(8,128)(2,1)}), bf16[64,160,128]{2,1,0:T(8,128)(2,1)}, u32[]{:S(2)}, u32[]{:S(2)}) %all-to-all-start) | async-done | bytes 2621472 | tf_op jit(solution)/shard_map/all_to_all | solution.py:112
  138.8 6.5 %all-to-all-start.3 = ((bf16[64,240,128]{2,1,0:T(8,128)(2,1)}), bf16[64,240,128]{2,1,0:T(8,128)(2,1)}, u32[]{:S(2)}, u32[]{:S(2)}) async-start(bf16[64,240,128]{2,1,0:T(8,128)(2,1)} %pad_maximum_fusion.2), calls=%async_computation.3 | async-start | bytes 7864320 | tf_op jit(solution)/shard_map/all_to_all | solution.py:112
  183.6 10.4 %all-to-all-done.3 = bf16[64,240,128]{2,1,0:T(8,128)(2,1)} async-done(((bf16[64,240,128]{2,1,0:T(8,128)(2,1)}), bf16[64,240,128]{2,1,0:T(8,128)(2,1)}, u32[]{:S(2)}, u32[]{:S(2)}) %all-to-all-start.3) | async-done | bytes 3932192 | tf_op jit(solution)/shard_map/all_to_all | solution.py:112
  194.0 12.5 %all-to-all-start.1 = ((bf16[64,240,128]{2,1,0:T(8,128)(2,1)}), bf16[64,240,128]{2,1,0:T(8,128)(2,1)}, u32[]{:S(2)}, u32[]{:S(2)}) async-start(bf16[64,240,128]{2,1,0:T(8,128)(2,1)} %pad_maximum_fusion.1), calls=%async_computation.1 | async-start | bytes 7864320 | tf_op jit(solution)/shard_map/all_to_all | solution.py:112
  206.9 6.0 %fusion.95 = f32[2048,768]{1,0:T(8,128)} fusion(bf16[320,2048]{1,0:T(8,128)(2,1)} %reshape.450, bf16[320,768]{1,0:T(8,128)(2,1)} %copy-done.42), kind=kOutput, calls=%fused_computation.174 | convolution fusion | flops 1006632960 | bytes 8093696 | tf_op jit(solution)/shard_map/dot_general | solution.py:97
  212.9 4.6 %fusion.96 = f32[2048,768]{1,0:T(8,128)} fusion(bf16[320,2048]{1,0:T(8,128)(2,1)S(1)} %copy-done.7, bf16[320,768]{1,0:T(8,128)(2,1)S(1)} %copy-done.41), kind=kOutput, calls=%fused_computation.175 | convolution fusion | flops 1006632960 | bytes 8093696 | tf_op jit(solution)/shard_map/dot_general | solution.py:97
  224.9 4.7 %fusion.7 = f32[320,768]{1,0:T(8,128)} fusion(bf16[320,2048]{1,0:T(8,128)(2,1)} %reshape.464, bf16[96,8,16,128]{3,2,1,0:T(8,128)(2,1)} %bitcast.235), kind=kOutput, calls=%fused_computation.33 | convolution fusion | flops 1006632960 | bytes 5439488 | tf_op jit(solution)/shard_map/dot_general | solution.py:18
  231.8 21.2 %all-to-all-done.1 = bf16[64,240,128]{2,1,0:T(8,128)(2,1)} async-done(((bf16[64,240,128]{2,1,0:T(8,128)(2,1)}), bf16[64,240,128]{2,1,0:T(8,128)(2,1)}, u32[]{:S(2)}, u32[]{:S(2)}) %all-to-all-start.1) | async-done | bytes 3932192 | tf_op jit(solution)/shard_map/all_to_all | solution.py:112
  252.9 4.2 fusion.86
  260.4 4.7 %fusion.9 = f32[320,768]{1,0:T(8,128)} fusion(bf16[320,2048]{1,0:T(8,128)(2,1)} %reshape.460, bf16[96,8,16,128]{3,2,1,0:T(8,128)(2,1)} %bitcast.236), kind=kOutput, calls=%fused_computation.35 | convolution fusion | flops 1006632960 | bytes 5439488 | tf_op jit(solution)/shard_map/dot_general | solution.py:18
  274.3 5.3 %multiply_convert_fusion.8 = (bf16[320,768]{1,0:T(8,128)(2,1)}, bf16[320,768]{1,0:T(8,128)(2,1)S(1)}) fusion(f32[320,768]{1,0:T(8,128)} %fusion.9, f32[320,768]{1,0:T(8,128)} %fusion.17, bf16[320,2048]{1,0:T(8,128)(2,1)} %reshape.459, bf16[96,8,16,128]{3,2,1,0:T(8,128)(2,1)} %bitcast.229), kind=kOutput, calls=%fused_computation.101 | convolution fusion | flops 1009827840 | bytes 7405568 | tf_op jit(solution)/shard_map/dot_general | solution.py:26
  290.2 4.7 %copy.46 = bf16[2048,768]{0,1:T(8,128)(2,1)} copy(bf16[2048,768]{1,0:T(8,128)(2,1)} %add_convert_fusion.2) | data formatting | bytes 6291456
  306.2 4.8 %copy.48 = bf16[2048,768]{0,1:T(8,128)(2,1)} copy(bf16[2048,768]{1,0:T(8,128)(2,1)} %add_convert_fusion.1) | data formatting | bytes 6291456
  319.1 5.8 %add_convert_fusion = bf16[768,2048]{1,0:T(8,128)(2,1)} fusion(f32[768,2048]{1,0:T(8,128)S(1)} %fusion.61, f32[768,2048]{1,0:T(8,128)S(1)} %fusion.59, f32[768,2048]{1,0:T(8,128)S(1)} %fusion.60, bf16[320,2048]{1,0:T(8,128)(2,1)S(1)} %copy-done.17, f32[320,768]{1,0:T(8,128)} %fusion.15, f32[320,768]{1,0:T(8,128)} %fusion.7), kind=kOutput, calls=%fused_computation.20 | convolution fusion | flops 1014398976 | bytes 25296896 | tf_op jit(solution)/shard_map/dot_general | solution.py:99
  332.9 10.6 %all-to-all-start.5 = ((bf16[64,80,128]{2,1,0:T(8,128)(2,1)}), bf16[64,80,128]{2,1,0:T(8,128)(2,1)}, u32[]{:S(2)}, u32[]{:S(2)}) async-start(bf16[64,80,128]{2,1,0:T(8,128)(2,1)} %reshape.465), calls=%async_computation.5 | async-start | bytes 2621440 | tf_op jit(solution)/shard_map/all_to_all | solution.py:112
  348.6 16.3 %all-to-all-done.5 = bf16[64,80,128]{2,1,0:T(8,128)(2,1)} async-done(((bf16[64,80,128]{2,1,0:T(8,128)(2,1)}), bf16[64,80,128]{2,1,0:T(8,128)(2,1)}, u32[]{:S(2)}, u32[]{:S(2)}) %all-to-all-start.5) | async-done | bytes 1310752 | tf_op jit(solution)/shard_map/all_to_all | solution.py:112
  365.0 4.7 %all-to-all-start.4 = ((bf16[64,80,128]{2,1,0:T(8,128)(2,1)}), bf16[64,80,128]{2,1,0:T(8,128)(2,1)S(1)}, u32[]{:S(2)}, u32[]{:S(2)}) async-start(bf16[64,80,128]{2,1,0:T(8,128)(2,1)} %reshape.461), calls=%async_computation.4 | async-start | bytes 2621440 | tf_op jit(solution)/shard_map/all_to_all | solution.py:112
  369.9 20.7 %all-to-all-done.4 = bf16[64,80,128]{2,1,0:T(8,128)(2,1)S(1)} async-done(((bf16[64,80,128]{2,1,0:T(8,128)(2,1)}), bf16[64,80,128]{2,1,0:T(8,128)(2,1)S(1)}, u32[]{:S(2)}, u32[]{:S(2)}) %all-to-all-start.4) | async-done | bytes 1310752 | tf_op jit(solution)/shard_map/all_to_all | solution.py:112
  390.6 4.8 %pad_maximum_fusion = bf16[64,20,16,128]{3,2,1,0:T(8,128)(2,1)} fusion(bf16[64,5,16,128]{3,2,1,0:T(8,128)(2,1)} %bitcast.17, bf16[64,5,16,128]{3,2,1,0:T(8,128)(2,1)S(1)} %bitcast.218, bf16[64,5,16,128]{3,2,1,0:T(8,128)(2,1)S(1)} %bitcast.225, bf16[64,5,16,128]{3,2,1,0:T(8,128)(2,1)} %bitcast.226), kind=kLoop, calls=%fused_computation.25 | loop fusion | flops 7864320 | bytes 10485760 | tf_op jit(solution)/shard_map/concatenate | solution.py:134
  395.4 10.9 %gather_fusion.8 = bf16[1024,16,128]{2,1,0:T(8,128)(2,1)} fusion(bf16[1280,16,128]{2,1,0:T(8,128)(2,1)} %bitcast.215, s32[1024]{0:T(1024)S(1)} %broadcast_clamp_fusion), kind=kCustom, calls=%fused_computation.8 | custom fusion | bytes 8392704 | tf_op jit(solution)/shard_map/gather | solution.py:137
  (294 shorter events, 206.8 us)
Async XLA Ops:
  12.8 25.7 %copy-start = (bf16[129,16,128]{2,1,0:T(8,128)(2,1)}, bf16[129,16,128]{2,1,0:T(8,128)(2,1)S(1)}, u32[]{:S(2)}) copy-start(bf16[129,16,128]{2,1,0:T(8,128)(2,1)S(1)} %concatenate.22) | copy-start | bytes 1585156
  13.2 27.7 %copy-start.1 = (bf16[129,16,128]{2,1,0:T(8,128)(2,1)}, bf16[129,16,128]{2,1,0:T(8,128)(2,1)S(1)}, u32[]{:S(2)}) copy-start(bf16[129,16,128]{2,1,0:T(8,128)(2,1)S(1)} %concatenate.21) | copy-start | bytes 1585156
  21.2 72.3 %all-to-all-start.2 = ((bf16[64,160,128]{2,1,0:T(8,128)(2,1)}), bf16[64,160,128]{2,1,0:T(8,128)(2,1)}, u32[]{:S(2)}, u32[]{:S(2)}) async-start(bf16[64,160,128]{2,1,0:T(8,128)(2,1)} %pad_maximum_fusion.4), calls=%async_computation.2 | async-start | bytes 5242880 | tf_op jit(solution)/shard_map/all_to_all | solution.py:112
  66.6 5.2 %copy-start.23 = (bf16[320,16,128]{2,1,0:T(8,128)(2,1)S(1)}, bf16[320,16,128]{2,1,0:T(8,128)(2,1)}, u32[]{:S(2)}) copy-start(bf16[320,16,128]{2,1,0:T(8,128)(2,1)} %gather_fusion.5) | copy-start | bytes 3932164
  66.7 9.9 %slice-start.4 = ((s8[6291456]{0:T(1024)(128)(4,1)}), s8[4194304]{0:T(1024)(128)(4,1)S(1)}, s32[]{:S(2)}) async-start(s8[6291456]{0:T(1024)(128)(4,1)} %bitcast.206), calls=%async_computation.16 | async-start | bytes 8388608
  71.8 4.8 %slice-start.5 = ((s8[6291456]{0:T(1024)(128)(4,1)}), s8[2097152]{0:T(1024)(128)(4,1)S(1)}, s32[]{:S(2)}) async-start(s8[6291456]{0:T(1024)(128)(4,1)} %bitcast.206), calls=%async_computation.17 | async-start | bytes 4194304
  93.5 45.3 %all-to-all-start = ((bf16[64,160,128]{2,1,0:T(8,128)(2,1)}), bf16[64,160,128]{2,1,0:T(8,128)(2,1)}, u32[]{:S(2)}, u32[]{:S(2)}) async-start(bf16[64,160,128]{2,1,0:T(8,128)(2,1)} %pad_maximum_fusion.3), calls=%async_computation | async-start | bytes 5242880 | tf_op jit(solution)/shard_map/all_to_all | solution.py:112
  138.8 55.2 %all-to-all-start.3 = ((bf16[64,240,128]{2,1,0:T(8,128)(2,1)}), bf16[64,240,128]{2,1,0:T(8,128)(2,1)}, u32[]{:S(2)}, u32[]{:S(2)}) async-start(bf16[64,240,128]{2,1,0:T(8,128)(2,1)} %pad_maximum_fusion.2), calls=%async_computation.3 | async-start | bytes 7864320 | tf_op jit(solution)/shard_map/all_to_all | solution.py:112
  194.0 58.9 %all-to-all-start.1 = ((bf16[64,240,128]{2,1,0:T(8,128)(2,1)}), bf16[64,240,128]{2,1,0:T(8,128)(2,1)}, u32[]{:S(2)}, u32[]{:S(2)}) async-start(bf16[64,240,128]{2,1,0:T(8,128)(2,1)} %pad_maximum_fusion.1), calls=%async_computation.1 | async-start | bytes 7864320 | tf_op jit(solution)/shard_map/all_to_all | solution.py:112
  206.6 204.0 %reduce-scatter.10.cloned.1.call-start = ((), (), s32[]{:S(2)}) async-start(), calls=%async_computation.10 | async-start | bytes 4718592
  206.9 6.0 %copy-start.7 = (bf16[320,2048]{1,0:T(8,128)(2,1)S(1)}, bf16[320,2048]{1,0:T(8,128)(2,1)}, u32[]{:S(2)}) copy-start(bf16[320,2048]{1,0:T(8,128)(2,1)} %reshape.456) | copy-start | bytes 3932164
  206.9 6.0 %copy-start.41 = (bf16[320,768]{1,0:T(8,128)(2,1)S(1)}, bf16[320,768]{1,0:T(8,128)(2,1)}, u32[]{:S(2)}) copy-start(bf16[320,768]{1,0:T(8,128)(2,1)} %copy-done.40) | copy-start | bytes 1474564
  274.2 6.1 %copy-start.11 = (bf16[320,2048]{1,0:T(8,128)(2,1)S(1)}, bf16[320,2048]{1,0:T(8,128)(2,1)}, u32[]{:S(2)}) copy-start(bf16[320,2048]{1,0:T(8,128)(2,1)} %reshape.460) | copy-start | bytes 3932164
  274.2 8.0 %copy-start.33 = (bf16[6,128,16,128]{3,2,1,0:T(8,128)(2,1)S(1)}, bf16[6,128,16,128]{3,2,1,0:T(8,128)(2,1)}, u32[]{:S(2)}) copy-start(bf16[6,128,16,128]{3,2,1,0:T(8,128)(2,1)} %fusion.4) | copy-start | bytes 9437188
  274.2 8.0 %copy-start.52 = (f32[320,768]{1,0:T(8,128)S(1)}, f32[320,768]{1,0:T(8,128)}, u32[]{:S(2)}) copy-start(f32[320,768]{1,0:T(8,128)} %fusion.15) | copy-start | bytes 2949124
  280.4 5.1 %slice-start = ((s8[6291456]{0:T(1024)(128)(4,1)}), s8[4194304]{0:T(1024)(128)(4,1)S(1)}, s32[]{:S(2)}) async-start(s8[6291456]{0:T(1024)(128)(4,1)} %bitcast.202), calls=%async_computation.12 | async-start | bytes 8388608
  280.4 5.1 %slice-start.2 = ((s8[6291456]{0:T(1024)(128)(4,1)}), s8[4194304]{0:T(1024)(128)(4,1)S(1)}, s32[]{:S(2)}) async-start(s8[6291456]{0:T(1024)(128)(4,1)} %bitcast.204), calls=%async_computation.14 | async-start | bytes 8388608
  295.0 118.2 %reduce-scatter.12.cloned.1.call-start = ((), (), s32[]{:S(2)}) async-start(), calls=%async_computation.11 | async-start | bytes 4718592
  311.1 104.7 %reduce-scatter.8.cloned.1.call-start = ((), (), s32[]{:S(2)}) async-start(), calls=%async_computation.9 | async-start | bytes 4718592 | tf_op jit(solution)/shard_map/reduce_scatter | solution.py:130
  332.9 32.1 %all-to-all-start.5 = ((bf16[64,80,128]{2,1,0:T(8,128)(2,1)}), bf16[64,80,128]{2,1,0:T(8,128)(2,1)}, u32[]{:S(2)}, u32[]{:S(2)}) async-start(bf16[64,80,128]{2,1,0:T(8,128)(2,1)} %reshape.465), calls=%async_computation.5 | async-start | bytes 2621440 | tf_op jit(solution)/shard_map/all_to_all | solution.py:112
  347.1 22.5 %copy-start.64 = (f32[1024]{0:T(1024)S(1)}, f32[1024]{0:T(1024)}, u32[]{:S(2)}) copy-start(f32[1024]{0:T(1024)} %copy-done.63) | copy-start | bytes 12292
  347.1 22.5 %copy-start.62 = (s32[128,8]{0,1:T(8,128)S(1)}, s32[128,8]{0,1:T(8,128)}, u32[]{:S(2)}) copy-start(s32[128,8]{0,1:T(8,128)} %param.14) | copy-start | bytes 12292
  347.2 43.4 %copy-start.25 = (bf16[64,80,128]{2,1,0:T(8,128)(2,1)S(1)}, bf16[64,80,128]{2,1,0:T(8,128)(2,1)}, u32[]{:S(2)}) copy-start(bf16[64,80,128]{2,1,0:T(8,128)(2,1)} %get-tuple-element.9) | copy-start | bytes 3932164
  365.0 25.6 %all-to-all-start.4 = ((bf16[64,80,128]{2,1,0:T(8,128)(2,1)}), bf16[64,80,128]{2,1,0:T(8,128)(2,1)S(1)}, u32[]{:S(2)}, u32[]{:S(2)}) async-start(bf16[64,80,128]{2,1,0:T(8,128)(2,1)} %reshape.461), calls=%async_computation.4 | async-start | bytes 2621440 | tf_op jit(solution)/shard_map/all_to_all | solution.py:112
  (62 other events, 165.9 us)
Sparse Core Ops, SparseCore 0:
  295.1 14.7 reduce-scatter.9
  312.4 14.9 reduce-scatter.11
  330.3 14.9 reduce-scatter.7

commit v3 on v2

--- a/solution.py
+++ b/solution.py
@@ -94,12 +94,9 @@
         row_input = jnp.dot(gate_grad, gate_w.T, preferred_element_type=jnp.float32)
         row_input = row_input + jnp.dot(up_grad, up_w.T, preferred_element_type=jnp.float32)
         back_rows = row_input.astype(jnp.bfloat16).reshape(experts, span, LANES)
-        part_gate = jnp.dot(xrows.T, gate_grad, preferred_element_type=jnp.float32)
-        part_up = jnp.dot(xrows.T, up_grad, preferred_element_type=jnp.float32)
-        part_down = jnp.dot(hidden.T, row_grad, preferred_element_type=jnp.float32)
-        return back_rows, (part_gate, part_up, part_down)
+        return back_rows, (xrows, row_grad, hidden, gate_grad, up_grad)
 
-    terms = None
+    saved = []
     arrived = [None] * chunks
     backs = [None] * chunks
     returned = [None] * chunks
@@ -117,9 +114,14 @@
         if step >= 2:
             returned[step - 2] = got[:, -span:]
         if 1 <= step <= chunks:
-            backs[step - 1], parts = compute(arrived[step - 1])
-            terms = parts if terms is None else tuple(a + b for a, b in zip(terms, parts))
-    term_gate, term_up, term_down = terms
+            backs[step - 1], kept = compute(arrived[step - 1])
+            saved.append(kept)
+    xrows, row_grad, hidden, gate_grad, up_grad = (
+        jnp.concatenate(list(group), axis=0) for group in zip(*saved)
+    )
+    term_gate = jnp.dot(xrows.T, gate_grad, preferred_element_type=jnp.float32)
+    term_up = jnp.dot(xrows.T, up_grad, preferred_element_type=jnp.float32)
+    term_down = jnp.dot(hidden.T, row_grad, preferred_element_type=jnp.float32)
     sum_gate, sum_up, sum_down = (
         lax.psum_scatter(
             term_gate.astype(jnp.bfloat16), "replica", scatter_dimension=1, tiled=True

time: 429 us -> 420 us (0.979)
  matrix products: 91.6 us -> 77.5 us
    dot_general x12 -> x3, matrix products: 40.4 us -> 25.7 us  [the longest x1 9.07 us: shards(): term_gate = jnp.dot(xrows.T, gate_grad, preferred_element_type=jnp.float32)]
    unnamed x172 -> x131, local copies, waits for them, and re-layouts: 50.5 us -> 52.5 us
  transfers between devices with their start and end apart: 9 -> 9, of which waited for: 5 -> 5; matrix products, arithmetic and copies ran while one was open for 49% -> 48% of each run, Pallas kernels for 0% -> 0%
where the time goes in v3:
time: 420 us; the launch traced here: 414 us
  local copies, waits for them, and re-layouts  140 us (33%)
  matrix products  77.5 us (18%)
  waiting for transfers between devices  76.1 us (18%)
  starting transfers between devices  58.4 us (14%)
  other arithmetic  46.5 us (11%)
  between operations  14.8 us (4%)
    all_to_all x6, waiting for transfers between devices, shards(): lax.all_to_all(jnp.concatenate(pieces, axis=1), 'expert', split_axis=0, c...  76.1 us
    all_to_all x6, starting transfers between devices, shards(): lax.all_to_all(jnp.concatenate(pieces, axis=1), 'expert', split_axis=0, c...  58.1 us
    unnamed x131, local copies, waits for them, and re-layouts  52.5 us
    convert_element_type x5, other arithmetic, dequant(): (blocks * scale[:, None, :, None]).reshape(rows, cols).astype(jnp.bfloat16)  17.3 us
    dot_general x4, matrix products, forward_parts(): pre_gate = jnp.dot(xrows, gate_w, preferred_element_type=jnp.float32)  13.3 us
    reshape x4, local copies, waits for them, and re-layouts, compute(): row_grad = got[:, span:2 * span].reshape(rows_in, width)  13.1 us
    reshape x4, local copies, waits for them, and re-layouts, compute(): xrows = got[:, :span].reshape(rows_in, width)  12.9 us
    dot_general x4, matrix products, unit_grads(): jnp.dot(row_grad, down_w.T, preferred_element_type=jnp.float32)  11.8 us
  transfers between devices with their start and end apart: 9, of which 5 were waited for; matrix products, arithmetic and copies ran while one was open for 48% of the time, Pallas kernels for 0%

profile of v3, /device:TPU:0, one launch (start us, length us, event | category | flops | bytes accessed | tf_op | source)
XLA Modules:
  0.0 413.8 jit_solution(636383031251850154)
XLA Ops:
  20.7 12.3 %all-to-all-start = ((bf16[64,160,128]{2,1,0:T(8,128)(2,1)}), bf16[64,160,128]{2,1,0:T(8,128)(2,1)}, u32[]{:S(2)}, u32[]{:S(2)}) async-start(bf16[64,160,128]{2,1,0:T(8,128)(2,1)} %pad_maximum_fusion.3), calls=%async_computation | async-start | bytes 5242880 | tf_op jit(solution)/shard_map/all_to_all | solution.py:109
  61.7 4.1 %copy.57 = f32[96,8,16,128]{3,2,1,0:T(8,128)} copy(f32[96,8,16,128]{3,1,2,0:T(8,128)S(1)} %convert_bitcast_fusion.3) | data formatting | bytes 12582912
  66.2 5.3 %multiply_convert_fusion = bf16[16,128,6,128]{1,0,3,2:T(8,128)(2,1)} fusion(f32[16,128,6,128]{1,0,3,2:T(8,128)} %bitcast.190, f32[16,6]{0,1:T(8,128)S(1)} %bitcast.231), kind=kLoop, calls=%fused_computation.20 | loop fusion | flops 3145728 | bytes 9437568 | tf_op jit(solution)/shard_map/convert_element_type | solution.py:14
  92.7 10.9 %all-to-all-start.2 = ((bf16[64,160,128]{2,1,0:T(8,128)(2,1)}), bf16[64,160,128]{2,1,0:T(8,128)(2,1)}, u32[]{:S(2)}, u32[]{:S(2)}) async-start(bf16[64,160,128]{2,1,0:T(8,128)(2,1)} %pad_maximum_fusion.4), calls=%async_computation.2 | async-start | bytes 5242880 | tf_op jit(solution)/shard_map/all_to_all | solution.py:109
  133.3 4.8 %all-to-all-done.2 = bf16[64,160,128]{2,1,0:T(8,128)(2,1)} async-done(((bf16[64,160,128]{2,1,0:T(8,128)(2,1)}), bf16[64,160,128]{2,1,0:T(8,128)(2,1)}, u32[]{:S(2)}, u32[]{:S(2)}) %all-to-all-start.2) | async-done | bytes 2621472 | tf_op jit(solution)/shard_map/all_to_all | solution.py:109
  138.1 6.7 %all-to-all-start.1 = ((bf16[64,240,128]{2,1,0:T(8,128)(2,1)}), bf16[64,240,128]{2,1,0:T(8,128)(2,1)}, u32[]{:S(2)}, u32[]{:S(2)}) async-start(bf16[64,240,128]{2,1,0:T(8,128)(2,1)} %pad_maximum_fusion.1), calls=%async_computation.1 | async-start | bytes 7864320 | tf_op jit(solution)/shard_map/all_to_all | solution.py:109
  183.6 9.8 %all-to-all-done.1 = bf16[64,240,128]{2,1,0:T(8,128)(2,1)} async-done(((bf16[64,240,128]{2,1,0:T(8,128)(2,1)}), bf16[64,240,128]{2,1,0:T(8,128)(2,1)}, u32[]{:S(2)}, u32[]{:S(2)}) %all-to-all-start.1) | async-done | bytes 3932192 | tf_op jit(solution)/shard_map/all_to_all | solution.py:109
  193.3 12.7 %all-to-all-start.3 = ((bf16[64,240,128]{2,1,0:T(8,128)(2,1)}), bf16[64,240,128]{2,1,0:T(8,128)(2,1)}, u32[]{:S(2)}, u32[]{:S(2)}) async-start(bf16[64,240,128]{2,1,0:T(8,128)(2,1)} %pad_maximum_fusion.2), calls=%async_computation.3 | async-start | bytes 7864320 | tf_op jit(solution)/shard_map/all_to_all | solution.py:109
  210.0 4.1 fusion.110
  220.7 4.7 %fusion.36 = f32[320,768]{1,0:T(8,128)} fusion(bf16[320,2048]{1,0:T(8,128)(2,1)} %reshape.459, bf16[96,8,16,128]{3,2,1,0:T(8,128)(2,1)} %bitcast.215), kind=kOutput, calls=%fused_computation.59 | convolution fusion | flops 1006632960 | bytes 5439488 | tf_op jit(solution)/shard_map/dot_general | solution.py:26
  227.6 24.8 %all-to-all-done.3 = bf16[64,240,128]{2,1,0:T(8,128)(2,1)} async-done(((bf16[64,240,128]{2,1,0:T(8,128)(2,1)}), bf16[64,240,128]{2,1,0:T(8,128)(2,1)}, u32[]{:S(2)}, u32[]{:S(2)}) %all-to-all-start.3) | async-done | bytes 3932192 | tf_op jit(solution)/shard_map/all_to_all | solution.py:109
  252.4 4.2 %fusion.111 = (bf16[64,80,128]{2,1,0:T(8,128)(2,1)}, bf16[64,80,128]{2,1,0:T(8,128)(2,1)}, bf16[64,80,128]{2,1,0:T(8,128)(2,1)}) fusion(bf16[64,240,128]{2,1,0:T(8,128)(2,1)} %all-to-all-done.3), kind=kLoop, calls=%fused_computation.195 | loop fusion | bytes 7864320 | tf_op jit(solution)/shard_map/slice | solution.py:115
  259.9 4.6 %fusion.34 = f32[320,768]{1,0:T(8,128)} fusion(bf16[320,2048]{1,0:T(8,128)(2,1)} %reshape.463, bf16[96,8,16,128]{3,2,1,0:T(8,128)(2,1)} %bitcast.216), kind=kOutput, calls=%fused_computation.57 | convolution fusion | flops 1006632960 | bytes 5439488 | tf_op jit(solution)/shard_map/dot_general | solution.py:26
  280.4 8.5 %convolution_convert_fusion = bf16[2048,768]{1,0:T(8,128)(2,1)} fusion(bf16[1280,2048]{1,0:T(8,128)(2,1)} %constant_dynamic-update-slice_fusion, bf16[320,768]{1,0:T(8,128)(2,1)S(1)} %get-tuple-element.27, bf16[320,768]{1,0:T(8,128)(2,1)S(1)} %get-tuple-element.24, bf16[320,768]{1,0:T(8,128)(2,1)S(1)} %copy-done.43, bf16[320,768]{1,0:T(8,128)(2,1)S(1)} %copy-done.41), kind=kOutput, calls=%fused_computation.39 | convolution fusion | flops 4035969024 | bytes 10354688 | tf_op jit(solution)/shard_map/dot_general | solution.py:123
  288.9 4.7 %copy.48 = bf16[2048,768]{0,1:T(8,128)(2,1)} copy(bf16[2048,768]{1,0:T(8,128)(2,1)} %convolution_convert_fusion) | data formatting | bytes 6291456
  293.9 9.1 %convolution_convert_fusion.1 = bf16[2048,768]{1,0:T(8,128)(2,1)} fusion(bf16[1280,2048]{1,0:T(8,128)(2,1)} %constant_dynamic-update-slice_fusion, bf16[320,768]{1,0:T(8,128)(2,1)} %get-tuple-element.26, bf16[320,768]{1,0:T(8,128)(2,1)} %get-tuple-element.23, bf16[320,768]{1,0:T(8,128)(2,1)} %copy-done.32, bf16[320,768]{1,0:T(8,128)(2,1)} %copy-done.31), kind=kOutput, calls=%fused_computation.40 | convolution fusion | flops 4035969024 | bytes 10354688 | tf_op jit(solution)/shard_map/dot_general | solution.py:122
  303.0 4.9 %copy.46 = bf16[2048,768]{0,1:T(8,128)(2,1)} copy(bf16[2048,768]{1,0:T(8,128)(2,1)} %convolution_convert_fusion.1) | data formatting | bytes 6291456
  307.9 8.1 %fusion.15 = bf16[768,2048]{1,0:T(8,128)(2,1)} fusion(bf16[320,2048]{1,0:T(8,128)(2,1)} %reshape.463, bf16[320,2048]{1,0:T(8,128)(2,1)} %reshape.459, bf16[320,2048]{1,0:T(8,128)(2,1)} %reshape.455, bf16[320,2048]{1,0:T(8,128)(2,1)} %reshape.449, bf16[320,768]{1,0:T(8,128)(2,1)} %get-tuple-element.25, bf16[320,768]{1,0:T(8,128)(2,1)} %get-tuple-element.22, ...), kind=kOutput, calls=%fused_computation.38 | convolution fusion | flops 4056940544 | bytes 10354688 | tf_op jit(solution)/shard_map/dot_general | solution.py:124
  324.2 10.7 %all-to-all-start.4 = ((bf16[64,80,128]{2,1,0:T(8,128)(2,1)}), bf16[64,80,128]{2,1,0:T(8,128)(2,1)}, u32[]{:S(2)}, u32[]{:S(2)}) async-start(bf16[64,80,128]{2,1,0:T(8,128)(2,1)} %reshape.461), calls=%async_computation.4 | async-start | bytes 2621440 | tf_op jit(solution)/shard_map/all_to_all | solution.py:109
  339.9 16.4 %all-to-all-done.4 = bf16[64,80,128]{2,1,0:T(8,128)(2,1)} async-done(((bf16[64,80,128]{2,1,0:T(8,128)(2,1)}), bf16[64,80,128]{2,1,0:T(8,128)(2,1)}, u32[]{:S(2)}, u32[]{:S(2)}) %all-to-all-start.4) | async-done | bytes 1310752 | tf_op jit(solution)/shard_map/all_to_all | solution.py:109
  356.4 4.9 %all-to-all-start.5 = ((bf16[64,80,128]{2,1,0:T(8,128)(2,1)}), bf16[64,80,128]{2,1,0:T(8,128)(2,1)S(1)}, u32[]{:S(2)}, u32[]{:S(2)}) async-start(bf16[64,80,128]{2,1,0:T(8,128)(2,1)} %reshape.465), calls=%async_computation.5 | async-start | bytes 2621440 | tf_op jit(solution)/shard_map/all_to_all | solution.py:109
  361.6 20.3 %all-to-all-done.5 = bf16[64,80,128]{2,1,0:T(8,128)(2,1)S(1)} async-done(((bf16[64,80,128]{2,1,0:T(8,128)(2,1)}), bf16[64,80,128]{2,1,0:T(8,128)(2,1)S(1)}, u32[]{:S(2)}, u32[]{:S(2)}) %all-to-all-start.5) | async-done | bytes 1310752 | tf_op jit(solution)/shard_map/all_to_all | solution.py:109
  381.9 4.8 %pad_maximum_fusion = bf16[64,20,16,128]{3,2,1,0:T(8,128)(2,1)} fusion(bf16[64,5,16,128]{3,2,1,0:T(8,128)(2,1)S(1)} %bitcast.196, bf16[64,5,16,128]{3,2,1,0:T(8,128)(2,1)} %bitcast.16, bf16[64,5,16,128]{3,2,1,0:T(8,128)(2,1)} %bitcast.204, bf16[64,5,16,128]{3,2,1,0:T(8,128)(2,1)S(1)} %bitcast.203), kind=kLoop, calls=%fused_computation.22 | loop fusion | flops 7864320 | bytes 10485760 | tf_op jit(solution)/shard_map/concatenate | solution.py:136
  386.7 10.9 %gather_fusion.8 = bf16[1024,16,128]{2,1,0:T(8,128)(2,1)} fusion(bf16[1280,16,128]{2,1,0:T(8,128)(2,1)} %bitcast.193, s32[1024]{0:T(1024)S(1)} %broadcast_clamp_fusion), kind=kCustom, calls=%fused_computation.8 | custom fusion | bytes 8392704 | tf_op jit(solution)/shard_map/gather | solution.py:139
  (243 shorter events, 186.8 us)
Async XLA Ops:
  7.2 4.5 %copy-start.29 = (bf16[128,2048]{1,0:T(8,128)(2,1)S(1)}, bf16[128,2048]{1,0:T(8,128)(2,1)}, u32[]{:S(2)}) copy-start(bf16[128,2048]{1,0:T(8,128)(2,1)} %param.11) | copy-start | bytes 1572868
  12.2 25.9 %copy-start = (bf16[129,16,128]{2,1,0:T(8,128)(2,1)}, bf16[129,16,128]{2,1,0:T(8,128)(2,1)S(1)}, u32[]{:S(2)}) copy-start(bf16[129,16,128]{2,1,0:T(8,128)(2,1)S(1)} %concatenate.37) | copy-start | bytes 1585156
  12.7 28.0 %copy-start.1 = (bf16[129,16,128]{2,1,0:T(8,128)(2,1)}, bf16[129,16,128]{2,1,0:T(8,128)(2,1)S(1)}, u32[]{:S(2)}) copy-start(bf16[129,16,128]{2,1,0:T(8,128)(2,1)S(1)} %concatenate.36) | copy-start | bytes 1585156
  20.7 72.1 %all-to-all-start = ((bf16[64,160,128]{2,1,0:T(8,128)(2,1)}), bf16[64,160,128]{2,1,0:T(8,128)(2,1)}, u32[]{:S(2)}, u32[]{:S(2)}) async-start(bf16[64,160,128]{2,1,0:T(8,128)(2,1)} %pad_maximum_fusion.3), calls=%async_computation | async-start | bytes 5242880 | tf_op jit(solution)/shard_map/all_to_all | solution.py:109
  52.8 4.1 copy-start.38
  61.7 4.2 %copy-start.39 = (f32[1,16,6]{1,0,2:T(1,128)S(1)}, f32[1,16,6]{1,0,2:T(1,128)}, u32[]{:S(2)}) copy-start(f32[1,16,6]{1,0,2:T(1,128)} %param.19) | copy-start | bytes 1156
  66.2 5.3 %copy-start.13 = (bf16[320,16,128]{2,1,0:T(8,128)(2,1)S(1)}, bf16[320,16,128]{2,1,0:T(8,128)(2,1)}, u32[]{:S(2)}) copy-start(bf16[320,16,128]{2,1,0:T(8,128)(2,1)} %gather_fusion.1) | copy-start | bytes 3932164
  66.2 9.7 %slice-start = ((s8[6291456]{0:T(1024)(128)(4,1)}), s8[4194304]{0:T(1024)(128)(4,1)S(1)}, s32[]{:S(2)}) async-start(s8[6291456]{0:T(1024)(128)(4,1)} %bitcast.184), calls=%async_computation.12 | async-start | bytes 8388608
  71.5 4.4 %slice-start.1 = ((s8[6291456]{0:T(1024)(128)(4,1)}), s8[2097152]{0:T(1024)(128)(4,1)S(1)}, s32[]{:S(2)}) async-start(s8[6291456]{0:T(1024)(128)(4,1)} %bitcast.184), calls=%async_computation.13 | async-start | bytes 4194304
  92.7 45.3 %all-to-all-start.2 = ((bf16[64,160,128]{2,1,0:T(8,128)(2,1)}), bf16[64,160,128]{2,1,0:T(8,128)(2,1)}, u32[]{:S(2)}, u32[]{:S(2)}) async-start(bf16[64,160,128]{2,1,0:T(8,128)(2,1)} %pad_maximum_fusion.4), calls=%async_computation.2 | async-start | bytes 5242880 | tf_op jit(solution)/shard_map/all_to_all | solution.py:109
  138.1 55.3 %all-to-all-start.1 = ((bf16[64,240,128]{2,1,0:T(8,128)(2,1)}), bf16[64,240,128]{2,1,0:T(8,128)(2,1)}, u32[]{:S(2)}, u32[]{:S(2)}) async-start(bf16[64,240,128]{2,1,0:T(8,128)(2,1)} %pad_maximum_fusion.1), calls=%async_computation.1 | async-start | bytes 7864320 | tf_op jit(solution)/shard_map/all_to_all | solution.py:109
  193.3 59.0 %all-to-all-start.3 = ((bf16[64,240,128]{2,1,0:T(8,128)(2,1)}), bf16[64,240,128]{2,1,0:T(8,128)(2,1)}, u32[]{:S(2)}, u32[]{:S(2)}) async-start(bf16[64,240,128]{2,1,0:T(8,128)(2,1)} %pad_maximum_fusion.2), calls=%async_computation.3 | async-start | bytes 7864320 | tf_op jit(solution)/shard_map/all_to_all | solution.py:109
  206.0 195.8 %reduce-scatter.12.cloned.1.call-start = ((), (), s32[]{:S(2)}) async-start(), calls=%async_computation.11 | async-start | bytes 4718592
  220.7 4.7 %copy-start.10 = (bf16[320,2048]{1,0:T(8,128)(2,1)S(1)}, bf16[320,2048]{1,0:T(8,128)(2,1)}, u32[]{:S(2)}) copy-start(bf16[320,2048]{1,0:T(8,128)(2,1)} %reshape.460) | copy-start | bytes 3932164
  220.7 4.7 %copy-start.24 = (bf16[16,128,6,128]{1,0,3,2:T(8,128)(2,1)S(1)}, bf16[16,128,6,128]{1,0,3,2:T(8,128)(2,1)}, u32[]{:S(2)}) copy-start(bf16[16,128,6,128]{1,0,3,2:T(8,128)(2,1)} %multiply_convert_fusion) | copy-start | bytes 9437188
  267.7 6.7 %copy-start.48 = (f32[320,768]{1,0:T(8,128)S(1)}, f32[320,768]{1,0:T(8,128)}, u32[]{:S(2)}) copy-start(f32[320,768]{1,0:T(8,128)} %fusion.36) | copy-start | bytes 2949124
  267.7 6.7 %copy-start.49 = (f32[320,768]{1,0:T(8,128)S(1)}, f32[320,768]{1,0:T(8,128)}, u32[]{:S(2)}) copy-start(f32[320,768]{1,0:T(8,128)} %fusion.20) | copy-start | bytes 2949124
  293.6 110.8 %reduce-scatter.10.cloned.1.call-start = ((), (), s32[]{:S(2)}) async-start(), calls=%async_computation.10 | async-start | bytes 4718592
  307.9 99.1 %reduce-scatter.8.cloned.1.call-start = ((), (), s32[]{:S(2)}) async-start(), calls=%async_computation.9 | async-start | bytes 4718592 | tf_op jit(solution)/shard_map/reduce_scatter | solution.py:132
  324.2 32.2 %all-to-all-start.4 = ((bf16[64,80,128]{2,1,0:T(8,128)(2,1)}), bf16[64,80,128]{2,1,0:T(8,128)(2,1)}, u32[]{:S(2)}, u32[]{:S(2)}) async-start(bf16[64,80,128]{2,1,0:T(8,128)(2,1)} %reshape.461), calls=%async_computation.4 | async-start | bytes 2621440 | tf_op jit(solution)/shard_map/all_to_all | solution.py:109
  338.4 22.8 %copy-start.35 = (f32[1024]{0:T(1024)S(1)}, f32[1024]{0:T(1024)}, u32[]{:S(2)}) copy-start(f32[1024]{0:T(1024)} %copy-done.34) | copy-start | bytes 12292
  338.4 22.9 %copy-start.33 = (s32[128,8]{0,1:T(8,128)S(1)}, s32[128,8]{0,1:T(8,128)}, u32[]{:S(2)}) copy-start(s32[128,8]{0,1:T(8,128)} %param.14) | copy-start | bytes 12292
  338.5 43.4 %copy-start.15 = (bf16[64,80,128]{2,1,0:T(8,128)(2,1)S(1)}, bf16[64,80,128]{2,1,0:T(8,128)(2,1)}, u32[]{:S(2)}) copy-start(bf16[64,80,128]{2,1,0:T(8,128)(2,1)} %get-tuple-element.6) | copy-start | bytes 3932164
  356.4 25.5 %all-to-all-start.5 = ((bf16[64,80,128]{2,1,0:T(8,128)(2,1)}), bf16[64,80,128]{2,1,0:T(8,128)(2,1)S(1)}, u32[]{:S(2)}, u32[]{:S(2)}) async-start(bf16[64,80,128]{2,1,0:T(8,128)(2,1)} %reshape.465), calls=%async_computation.5 | async-start | bytes 2621440 | tf_op jit(solution)/shard_map/all_to_all | solution.py:109
  (40 other events, 100.9 us)
Sparse Core Ops, SparseCore 0:
  293.7 14.9 reduce-scatter.11
  311.2 14.9 reduce-scatter.9
  329.1 14.9 reduce-scatter.7

commit v4 on v3

--- a/solution.py
+++ b/solution.py
@@ -50,7 +50,7 @@
     used = got[:, 1] > 0.5
     table = jnp.where(used, got[:, 0], float(tok_rows)).astype(jnp.int32)
     gate_table = (got[:, 2] * 128.0 + got[:, 3]) / 65536.0
-    return dest, table, gate_table
+    return flat_ids, slot_of, table, gate_table
 
 
 def shards(
@@ -64,7 +64,7 @@
     per = capacity // chunks
     sub = width // LANES
     blk_width = width // x_scale.shape[1]
-    dest, table, gate_table = routing(expert_ids, gate_fixed, experts, capacity)
+    flat_ids, slot_of, table, gate_table = routing(expert_ids, gate_fixed, experts, capacity)
     scaled = x_quant.reshape(tok_rows, -1, blk_width).astype(jnp.float32) * x_scale[:, :, None]
     inputs = scaled.reshape(tok_rows, sub, LANES).astype(jnp.bfloat16)
     zero_row = jnp.zeros((1, sub, LANES), jnp.bfloat16)
@@ -119,29 +119,39 @@
     xrows, row_grad, hidden, gate_grad, up_grad = (
         jnp.concatenate(list(group), axis=0) for group in zip(*saved)
     )
-    term_gate = jnp.dot(xrows.T, gate_grad, preferred_element_type=jnp.float32)
-    term_up = jnp.dot(xrows.T, up_grad, preferred_element_type=jnp.float32)
-    term_down = jnp.dot(hidden.T, row_grad, preferred_element_type=jnp.float32)
-    sum_gate, sum_up, sum_down = (
-        lax.psum_scatter(
-            term_gate.astype(jnp.bfloat16), "replica", scatter_dimension=1, tiled=True
-        ).astype(jnp.float32),
-        lax.psum_scatter(
-            term_up.astype(jnp.bfloat16), "replica", scatter_dimension=1, tiled=True
-        ).astype(jnp.float32),
-        lax.psum_scatter(
-            term_down.astype(jnp.bfloat16), "replica", scatter_dimension=0, tiled=True
-        ).astype(jnp.float32),
+    ff = gate_grad.shape[1]
+    half = ff // lax.axis_size("replica")
+    mine = lax.axis_index("replica")
+    other = 1 - mine
+
+    def cols(a, r):
+        return lax.dynamic_slice_in_dim(a, r * half, half, axis=1)
+
+    def weight_parts(r):
+        part_gate = jnp.dot(xrows.T, cols(gate_grad, r), preferred_element_type=jnp.float32)
+        part_up = jnp.dot(xrows.T, cols(up_grad, r), preferred_element_type=jnp.float32)
+        part_down = jnp.dot(cols(hidden, r).T, row_grad, preferred_element_type=jnp.float32)
+        return tuple(p.astype(jnp.bfloat16) for p in (part_gate, part_up, part_down))
+
+    sent = weight_parts(other)
+    kept = weight_parts(mine)
+    swap = [(0, 1), (1, 0)]
+    came = tuple(lax.ppermute(p, "replica", swap) for p in sent)
+    grad_gate, grad_up, grad_down = (
+        (k.astype(jnp.float32) + c.astype(jnp.float32)).astype(jnp.bfloat16)[None]
+        for k, c in zip(kept, came)
     )
-    back = jnp.concatenate(
-        [r.reshape(experts, per, sub, LANES) for r in returned], axis=1
-    ).reshape(experts * capacity, sub, LANES)
-    picked = back[dest].astype(jnp.float32)
-    grad_input = jnp.sum(picked.reshape(tok_rows, topk, sub, LANES), axis=1)
-    grad_input = grad_input.reshape(tok_rows, width).astype(jnp.bfloat16)
-    grad_gate = sum_gate.astype(jnp.bfloat16)[None]
-    grad_up = sum_up.astype(jnp.bfloat16)[None]
-    grad_down = sum_down.astype(jnp.bfloat16)[None]
+    total = None
+    for c in range(chunks):
+        in_chunk = (slot_of // per) == c
+        col = jnp.where(in_chunk, flat_ids * per + slot_of % per, -1)
+        spots = jnp.arange(rows_in, dtype=jnp.int32)
+        hit = (col[:, None] == spots[None, :]).astype(jnp.bfloat16)
+        gather_mat = jnp.sum(hit.reshape(tok_rows, topk, rows_in), axis=1)
+        back3 = returned[c].reshape(rows_in, sub, LANES)
+        part = jnp.einsum("tj,jkl->tkl", gather_mat, back3, preferred_element_type=jnp.float32)
+        total = part if total is None else total + part
+    grad_input = total.reshape(tok_rows, width).astype(jnp.bfloat16)
     return (grad_input, grad_gate, grad_up, grad_down)
 
 

time: 420 us -> 376 us (0.90)
  waiting for transfers between devices: 76.1 us -> 41.1 us
  matrix products: 77.5 us -> 93.7 us
  local copies, waits for them, and re-layouts: 140 us -> 125 us
  between operations: 14.8 us -> 1.88 us
  starting transfers between devices: 58.4 us -> 63.7 us
    all_to_all x6, waiting for transfers between devices: 76.1 us -> 41.1 us  [shards(): lax.all_to_all(jnp.concatenate(pieces, axis=1), 'expert', split_axis=0, c...]
    dot_general x3 -> x10, matrix products: 25.7 us -> 41.5 us  [the longest x2 14.2 us: weight_parts(): jnp.dot(xrows.T, cols(gate_grad, r), preferred_element_type=jnp.float32)]
    gather x1 -> x0, local copies, waits for them, and re-layouts: 10.9 us -> none  [shards(): picked = back[dest].astype(jnp.float32)]
    slice x2 -> x0, local copies, waits for them, and re-layouts: 8.36 us -> none  [shards(): returned[step - 2] = got[:, -span:]]
    slice x2 -> x4, local copies, waits for them, and re-layouts: 6.77 us -> 15.1 us  [compute(): row_grad = got[:, span:2 * span].reshape(rows_in, width)]
    unnamed x131 -> x170, local copies, waits for them, and re-layouts: 52.5 us -> 45.6 us
    all_to_all x6, starting transfers between devices: 58.1 us -> 63 us  [shards(): lax.all_to_all(jnp.concatenate(pieces, axis=1), 'expert', split_axis=0, c...]
    dot_general x4, matrix products: 11.8 us -> 7.48 us  [unit_grads(): jnp.dot(row_grad, down_w.T, preferred_element_type=jnp.float32)]
  transfers between devices with their start and end apart: 9 -> 9, of which waited for: 5 -> 4; matrix products, arithmetic and copies ran while one was open for 48% -> 53% of each run, Pallas kernels for 0% -> 0%
where the time goes in v4:
time: 376 us; the launch traced here: 369 us
  local copies, waits for them, and re-layouts  125 us (33%)
  matrix products  93.7 us (25%)
  starting transfers between devices  63.7 us (17%)
  other arithmetic  43.7 us (12%)
  waiting for transfers between devices  41.1 us (11%)
    all_to_all x6, starting transfers between devices, shards(): lax.all_to_all(jnp.concatenate(pieces, axis=1), 'expert', split_axis=0, c...  63 us
    unnamed x170, local copies, waits for them, and re-layouts  45.6 us
    all_to_all x6, waiting for transfers between devices, shards(): lax.all_to_all(jnp.concatenate(pieces, axis=1), 'expert', split_axis=0, c...  41.1 us
    convert_element_type x5, other arithmetic, dequant(): (blocks * scale[:, None, :, None]).reshape(rows, cols).astype(jnp.bfloat16)  17.1 us
    dot_general x4, matrix products, forward_parts(): pre_gate = jnp.dot(xrows, gate_w, preferred_element_type=jnp.float32)  15.5 us
    slice x4, local copies, waits for them, and re-layouts, compute(): row_grad = got[:, span:2 * span].reshape(rows_in, width)  15.1 us
    dot_general x2, matrix products, weight_parts(): jnp.dot(xrows.T, cols(gate_grad, r), preferred_element_type=jnp.float32)  14.2 us
    reshape x4, local copies, waits for them, and re-layouts, compute(): row_grad = got[:, span:2 * span].reshape(rows_in, width)  13.3 us
  transfers between devices with their start and end apart: 9, of which 4 were waited for; matrix products, arithmetic and copies ran while one was open for 53% of the time, Pallas kernels for 0%

profile of v4, /device:TPU:0, one launch (start us, length us, event | category | flops | bytes accessed | tf_op | source)
XLA Modules:
  0.0 369.3 jit_solution(8700432246298838961)
XLA Ops:
  14.0 11.9 %all-to-all-start = ((bf16[64,160,128]{2,1,0:T(8,128)(2,1)}), bf16[64,160,128]{2,1,0:T(8,128)(2,1)}, u32[]{:S(2)}, u32[]{:S(2)}) async-start(bf16[64,160,128]{2,1,0:T(8,128)(2,1)} %pad_maximum_fusion.2), calls=%async_computation | async-start | bytes 5242880 | tf_op jit(solution)/shard_map/all_to_all | solution.py:109
  41.0 4.0 %copy.76 = f32[96,8,16,128]{3,2,1,0:T(8,128)} copy(f32[96,8,16,128]{3,1,2,0:T(8,128)S(1)} %convert_bitcast_fusion.1) | data formatting | bytes 12582912
  45.9 4.1 %copy.72 = f32[96,8,16,128]{3,2,1,0:T(8,128)} copy(f32[96,8,16,128]{3,1,2,0:T(8,128)S(1)} %convert_bitcast_fusion.4) | data formatting | bytes 12582912
  54.9 4.2 %copy.74 = f32[96,8,16,128]{3,2,1,0:T(8,128)} copy(f32[96,8,16,128]{3,1,2,0:T(8,128)S(1)} %convert_bitcast_fusion.3) | data formatting | bytes 12582912
  59.6 5.2 %multiply_convert_fusion = bf16[16,128,6,128]{1,0,3,2:T(8,128)(2,1)} fusion(f32[16,128,6,128]{1,0,3,2:T(8,128)} %bitcast.197, f32[16,6]{0,1:T(8,128)S(1)} %bitcast.233), kind=kLoop, calls=%fused_computation.19 | loop fusion | flops 3145728 | bytes 9437568 | tf_op jit(solution)/shard_map/convert_element_type | solution.py:14
  82.1 4.0 %fusion.1 = bf16[2048,768]{0,1:T(8,128)(2,1)} fusion(bf16[1,2048,768]{1,2,0:T(8,128)(2,1)S(1)} %copy-done.5, f32[96,8,16,128]{3,2,1,0:T(8,128)S(1)} %bitcast.199), kind=kLoop, calls=%fused_computation.13 | loop fusion | flops 4718592 | bytes 12582912 | tf_op jit(solution)/shard_map/convert_element_type | solution.py:14
  86.1 11.1 %all-to-all-start.2 = ((bf16[64,160,128]{2,1,0:T(8,128)(2,1)}), bf16[64,160,128]{2,1,0:T(8,128)(2,1)}, u32[]{:S(2)}, u32[]{:S(2)}) async-start(bf16[64,160,128]{2,1,0:T(8,128)(2,1)} %pad_maximum_fusion.3), calls=%async_computation.2 | async-start | bytes 5242880 | tf_op jit(solution)/shard_map/all_to_all | solution.py:109
  126.8 4.8 %all-to-all-done.2 = bf16[64,160,128]{2,1,0:T(8,128)(2,1)} async-done(((bf16[64,160,128]{2,1,0:T(8,128)(2,1)}), bf16[64,160,128]{2,1,0:T(8,128)(2,1)}, u32[]{:S(2)}, u32[]{:S(2)}) %all-to-all-start.2) | async-done | bytes 2621472 | tf_op jit(solution)/shard_map/all_to_all | solution.py:109
  131.6 6.5 %all-to-all-start.1 = ((bf16[64,240,128]{2,1,0:T(8,128)(2,1)}), bf16[64,240,128]{2,1,0:T(8,128)(2,1)}, u32[]{:S(2)}, u32[]{:S(2)}) async-start(bf16[64,240,128]{2,1,0:T(8,128)(2,1)} %pad_maximum_fusion), calls=%async_computation.1 | async-start | bytes 7864320 | tf_op jit(solution)/shard_map/all_to_all | solution.py:109
  177.9 8.8 %all-to-all-done.1 = bf16[64,240,128]{2,1,0:T(8,128)(2,1)} async-done(((bf16[64,240,128]{2,1,0:T(8,128)(2,1)}), bf16[64,240,128]{2,1,0:T(8,128)(2,1)}, u32[]{:S(2)}, u32[]{:S(2)}) %all-to-all-start.1) | async-done | bytes 3932192 | tf_op jit(solution)/shard_map/all_to_all | solution.py:109
  186.7 12.9 %all-to-all-start.3 = ((bf16[64,240,128]{2,1,0:T(8,128)(2,1)}), bf16[64,240,128]{2,1,0:T(8,128)(2,1)}, u32[]{:S(2)}, u32[]{:S(2)}) async-start(bf16[64,240,128]{2,1,0:T(8,128)(2,1)} %pad_maximum_fusion.1), calls=%async_computation.3 | async-start | bytes 7864320 | tf_op jit(solution)/shard_map/all_to_all | solution.py:109
  207.6 4.1 %fusion.113 = (bf16[64,80,128]{2,1,0:T(8,128)(2,1)}, bf16[64,80,128]{2,1,0:T(8,128)(2,1)}, bf16[64,80,128]{2,1,0:T(8,128)(2,1)}) fusion(bf16[64,240,128]{2,1,0:T(8,128)(2,1)} %all-to-all-done.1), kind=kLoop, calls=%fused_computation.221 | loop fusion | bytes 7864320 | tf_op jit(solution)/shard_map/slice | solution.py:90
  230.4 15.6 %all-to-all-done.3 = bf16[64,240,128]{2,1,0:T(8,128)(2,1)} async-done(((bf16[64,240,128]{2,1,0:T(8,128)(2,1)}), bf16[64,240,128]{2,1,0:T(8,128)(2,1)}, u32[]{:S(2)}, u32[]{:S(2)}) %all-to-all-start.3) | async-done | bytes 3932192 | tf_op jit(solution)/shard_map/all_to_all | solution.py:109
  246.0 4.2 %fusion.112 = (bf16[64,80,128]{2,1,0:T(8,128)(2,1)}, bf16[64,80,128]{2,1,0:T(8,128)(2,1)}, bf16[64,80,128]{2,1,0:T(8,128)(2,1)}) fusion(bf16[64,240,128]{2,1,0:T(8,128)(2,1)} %all-to-all-done.3), kind=kLoop, calls=%fused_computation.220 | loop fusion | bytes 7864320 | tf_op jit(solution)/shard_map/slice | solution.py:90
  253.4 4.5 %fusion.7 = f32[320,768]{1,0:T(8,128)} fusion(bf16[320,2048]{1,0:T(8,128)(2,1)} %reshape.510, bf16[96,8,16,128]{3,2,1,0:T(8,128)(2,1)} %bitcast.215), kind=kOutput, calls=%fused_computation.27 | convolution fusion | flops 1006632960 | bytes 5439488 | tf_op jit(solution)/shard_map/dot_general | solution.py:18
  276.1 10.3 %all-to-all-start.4 = ((bf16[64,80,128]{2,1,0:T(8,128)(2,1)}), bf16[64,80,128]{2,1,0:T(8,128)(2,1)S(1)}, u32[]{:S(2)}, u32[]{:S(2)}) async-start(bf16[64,80,128]{2,1,0:T(8,128)(2,1)} %reshape.507), calls=%async_computation.4 | async-start | bytes 2621440 | tf_op jit(solution)/shard_map/all_to_all | solution.py:109
  299.4 6.7 %convolution_convert_fusion.4 = bf16[2048,384]{1,0:T(8,128)(2,1)} fusion(bf16[1280,2048]{1,0:T(8,128)(2,1)} %constant_dynamic-update-slice_fusion, bf16[1280,768]{1,0:T(8,128)(2,1)S(1)} %copy-done.38, s32[]{:T(128)S(6)} %select_n.159), kind=kOutput, calls=%fused_computation.62 | convolution fusion | flops 2014052352 | bytes 7798788 | tf_op jit(solution)/shard_map/dot_general | solution.py:131
  306.2 4.1 %convolution_convert_fusion.2 = bf16[2048,384]{1,0:T(8,128)(2,1)} fusion(bf16[1280,2048]{1,0:T(8,128)(2,1)S(1)} %copy-done.62, bf16[1280,768]{1,0:T(8,128)(2,1)S(1)} %copy-done.39, s32[]{:T(128)S(6)} %select_n.159), kind=kOutput, calls=%fused_computation.60 | convolution fusion | flops 2014052352 | bytes 7798788 | tf_op jit(solution)/shard_map/dot_general | solution.py:132
  314.5 10.4 %all-to-all-start.5 = ((bf16[64,80,128]{2,1,0:T(8,128)(2,1)}), bf16[64,80,128]{2,1,0:T(8,128)(2,1)S(1)}, u32[]{:S(2)}, u32[]{:S(2)}) async-start(bf16[64,80,128]{2,1,0:T(8,128)(2,1)} %reshape.511), calls=%async_computation.5 | async-start | bytes 2621440 | tf_op jit(solution)/shard_map/all_to_all | solution.py:109
  324.9 6.3 %convolution_convert_fusion = bf16[384,2048]{1,0:T(8,128)(2,1)} fusion(bf16[1280,2048]{1,0:T(8,128)(2,1)} %constant_dynamic-update-slice_fusion.4, bf16[1280,768]{1,0:T(8,128)(2,1)} %pad_maximum_fusion.6, s32[]{:T(128)S(6)} %select_n.159), kind=kOutput, calls=%fused_computation.58 | convolution fusion | flops 2014052352 | bytes 7798788 | tf_op jit(solution)/shard_map/dot_general | solution.py:133
  335.0 11.8 %all-to-all-done.5 = bf16[64,80,128]{2,1,0:T(8,128)(2,1)S(1)} async-done(((bf16[64,80,128]{2,1,0:T(8,128)(2,1)}), bf16[64,80,128]{2,1,0:T(8,128)(2,1)S(1)}, u32[]{:S(2)}, u32[]{:S(2)}) %all-to-all-start.5) | async-done | bytes 1310752 | tf_op jit(solution)/shard_map/all_to_all | solution.py:109
  349.9 7.4 %fusion.40 = bf16[1,2048,384]{2,1,0:T(8,128)(2,1)} fusion(bf16[2048,384]{1,0:T(8,128)(2,1)} %collective-permute-done, bf16[1280,2048]{1,0:T(8,128)(2,1)} %constant_dynamic-update-slice_fusion, bf16[1280,768]{1,0:T(8,128)(2,1)} %pad_maximum_fusion.4, s32[]{:T(128)S(6)} %select_n.158), kind=kOutput, calls=%fused_computation.79 | convolution fusion | flops 2017198080 | bytes 9371652 | tf_op jit(solution)/shard_map/dot_general | solution.py:131
  357.4 5.3 %fusion.41 = bf16[1,2048,384]{2,1,0:T(8,128)(2,1)} fusion(bf16[2048,384]{1,0:T(8,128)(2,1)} %collective-permute-done.1, bf16[1280,2048]{1,0:T(8,128)(2,1)S(1)} %bitcast.228, bf16[1280,768]{1,0:T(8,128)(2,1)S(1)} %copy-done.40, s32[]{:T(128)S(6)} %select_n.158), kind=kOutput, calls=%fused_computation.80 | convolution fusion | flops 2017198080 | bytes 9371652 | tf_op jit(solution)/shard_map/dot_general | solution.py:132
  362.7 6.4 %fusion.42 = bf16[1,384,2048]{2,1,0:T(8,128)(2,1)} fusion(bf16[384,2048]{1,0:T(8,128)(2,1)} %collective-permute-done.2, bf16[1280,2048]{1,0:T(8,128)(2,1)} %constant_dynamic-update-slice_fusion.4, bf16[1280,768]{1,0:T(8,128)(2,1)S(1)} %copy-done.41, s32[]{:T(128)S(6)} %select_n.158), kind=kOutput, calls=%fused_computation.81 | convolution fusion | flops 2017198080 | bytes 9371652 | tf_op jit(solution)/shard_map/dot_general | solution.py:133
  (298 shorter events, 192.8 us)
Async XLA Ops:
  5.6 25.6 %copy-start = (bf16[129,16,128]{2,1,0:T(8,128)(2,1)}, bf16[129,16,128]{2,1,0:T(8,128)(2,1)S(1)}, u32[]{:S(2)}) copy-start(bf16[129,16,128]{2,1,0:T(8,128)(2,1)S(1)} %concatenate.34) | copy-start | bytes 1585156
  6.1 27.6 %copy-start.1 = (bf16[129,16,128]{2,1,0:T(8,128)(2,1)}, bf16[129,16,128]{2,1,0:T(8,128)(2,1)S(1)}, u32[]{:S(2)}) copy-start(bf16[129,16,128]{2,1,0:T(8,128)(2,1)S(1)} %concatenate.33) | copy-start | bytes 1585156
  14.0 72.1 %all-to-all-start = ((bf16[64,160,128]{2,1,0:T(8,128)(2,1)}), bf16[64,160,128]{2,1,0:T(8,128)(2,1)}, u32[]{:S(2)}, u32[]{:S(2)}) async-start(bf16[64,160,128]{2,1,0:T(8,128)(2,1)} %pad_maximum_fusion.2), calls=%async_computation | async-start | bytes 5242880 | tf_op jit(solution)/shard_map/all_to_all | solution.py:109
  59.6 9.7 %slice-start = ((s8[6291456]{0:T(1024)(128)(4,1)}), s8[4194304]{0:T(1024)(128)(4,1)S(1)}, s32[]{:S(2)}) async-start(s8[6291456]{0:T(1024)(128)(4,1)} %bitcast.191), calls=%async_computation.6 | async-start | bytes 8388608
  86.1 45.5 %all-to-all-start.2 = ((bf16[64,160,128]{2,1,0:T(8,128)(2,1)}), bf16[64,160,128]{2,1,0:T(8,128)(2,1)}, u32[]{:S(2)}, u32[]{:S(2)}) async-start(bf16[64,160,128]{2,1,0:T(8,128)(2,1)} %pad_maximum_fusion.3), calls=%async_computation.2 | async-start | bytes 5242880 | tf_op jit(solution)/shard_map/all_to_all | solution.py:109
  131.6 55.1 %all-to-all-start.1 = ((bf16[64,240,128]{2,1,0:T(8,128)(2,1)}), bf16[64,240,128]{2,1,0:T(8,128)(2,1)}, u32[]{:S(2)}, u32[]{:S(2)}) async-start(bf16[64,240,128]{2,1,0:T(8,128)(2,1)} %pad_maximum_fusion), calls=%async_computation.1 | async-start | bytes 7864320 | tf_op jit(solution)/shard_map/all_to_all | solution.py:109
  138.1 6.4 %copy-start.63 = (s32[128,8]{0,1:T(8,128)S(1)}, s32[128,8]{0,1:T(8,128)}, u32[]{:S(2)}) copy-start(s32[128,8]{0,1:T(8,128)} %param.14) | copy-start | bytes 12292
  186.7 59.3 %all-to-all-start.3 = ((bf16[64,240,128]{2,1,0:T(8,128)(2,1)}), bf16[64,240,128]{2,1,0:T(8,128)(2,1)}, u32[]{:S(2)}, u32[]{:S(2)}) async-start(bf16[64,240,128]{2,1,0:T(8,128)(2,1)} %pad_maximum_fusion.1), calls=%async_computation.3 | async-start | bytes 7864320 | tf_op jit(solution)/shard_map/all_to_all | solution.py:109
  274.6 11.8 %copy-start.52 = (bf16[320,768]{1,0:T(8,128)(2,1)S(1)}, bf16[320,768]{1,0:T(8,128)(2,1)}, u32[]{:S(2)}) copy-start(bf16[320,768]{1,0:T(8,128)(2,1)} %copy-done.51) | copy-start | bytes 1474564
  274.6 11.8 %copy-start.55 = (bf16[320,768]{1,0:T(8,128)(2,1)S(1)}, bf16[320,768]{1,0:T(8,128)(2,1)}, u32[]{:S(2)}) copy-start(bf16[320,768]{1,0:T(8,128)(2,1)} %copy-done.54) | copy-start | bytes 1474564
  274.6 11.8 %copy-start.59 = (bf16[320,768]{1,0:T(8,128)(2,1)S(1)}, bf16[320,768]{1,0:T(8,128)(2,1)}, u32[]{:S(2)}) copy-start(bf16[320,768]{1,0:T(8,128)(2,1)} %get-tuple-element.42) | copy-start | bytes 1474564
  276.1 38.4 %all-to-all-start.4 = ((bf16[64,80,128]{2,1,0:T(8,128)(2,1)}), bf16[64,80,128]{2,1,0:T(8,128)(2,1)S(1)}, u32[]{:S(2)}, u32[]{:S(2)}) async-start(bf16[64,80,128]{2,1,0:T(8,128)(2,1)} %reshape.507), calls=%async_computation.4 | async-start | bytes 2621440 | tf_op jit(solution)/shard_map/all_to_all | solution.py:109
  299.4 6.7 %copy-start.39 = (bf16[1280,768]{1,0:T(8,128)(2,1)S(1)}, bf16[1280,768]{1,0:T(8,128)(2,1)}, u32[]{:S(2)}) copy-start(bf16[1280,768]{1,0:T(8,128)(2,1)} %pad_maximum_fusion.5) | copy-start | bytes 5898244
  299.4 6.7 %copy-start.62 = (bf16[1280,2048]{1,0:T(8,128)(2,1)S(1)}, bf16[1280,2048]{1,0:T(8,128)(2,1)}, u32[]{:S(2)}) copy-start(bf16[1280,2048]{1,0:T(8,128)(2,1)} %constant_dynamic-update-slice_fusion) | copy-start | bytes 15728644
  306.1 43.8 %collective-permute-start = (bf16[2048,384]{1,0:T(8,128)(2,1)}, bf16[2048,384]{1,0:T(8,128)(2,1)}, u32[]{:S(2)}, u32[]{:S(2)}) collective-permute-start(bf16[2048,384]{1,0:T(8,128)(2,1)} %convolution_convert_fusion.4), channel_id=1, source_target_pairs={{0,1},{1,0},{2,3},{3,2},{4,5},{5,4},{6,7},{7,6},{8,9},{9,8},{10,11... | collective-permute-start | bytes 4718600 | tf_op jit(solution)/shard_map/ppermute | solution.py:139
  310.2 47.1 %collective-permute-start.1 = (bf16[2048,384]{1,0:T(8,128)(2,1)}, bf16[2048,384]{1,0:T(8,128)(2,1)}, u32[]{:S(2)}, u32[]{:S(2)}) collective-permute-start(bf16[2048,384]{1,0:T(8,128)(2,1)} %convolution_convert_fusion.2), channel_id=1, source_target_pairs={{0,1},{1,0},{2,3},{3,2},{4,5},{5,4},{6,7},{7,6},{8,9},{9,8},{10,11... | collective-permute-start | bytes 4718600 | tf_op jit(solution)/shard_map/ppermute | solution.py:139
  314.5 32.4 %all-to-all-start.5 = ((bf16[64,80,128]{2,1,0:T(8,128)(2,1)}), bf16[64,80,128]{2,1,0:T(8,128)(2,1)S(1)}, u32[]{:S(2)}, u32[]{:S(2)}) async-start(bf16[64,80,128]{2,1,0:T(8,128)(2,1)} %reshape.511), calls=%async_computation.5 | async-start | bytes 2621440 | tf_op jit(solution)/shard_map/all_to_all | solution.py:109
  324.9 6.6 %copy-start.23 = (bf16[64,80,128]{2,1,0:T(8,128)(2,1)S(1)}, bf16[64,80,128]{2,1,0:T(8,128)(2,1)}, u32[]{:S(2)}) copy-start(bf16[64,80,128]{2,1,0:T(8,128)(2,1)} %get-tuple-element.26) | copy-start | bytes 3932164
  324.9 6.6 %copy-start.60 = (bf16[128,320]{0,1:T(8,128)(2,1)S(1)}, bf16[128,320]{0,1:T(8,128)(2,1)}, u32[]{:S(2)}) copy-start(bf16[128,320]{0,1:T(8,128)(2,1)} %fusion.83) | copy-start | bytes 245764
  331.2 31.5 %collective-permute-start.2 = (bf16[384,2048]{1,0:T(8,128)(2,1)}, bf16[384,2048]{1,0:T(8,128)(2,1)}, u32[]{:S(2)}, u32[]{:S(2)}) collective-permute-start(bf16[384,2048]{1,0:T(8,128)(2,1)} %convolution_convert_fusion), channel_id=1, source_target_pairs={{0,1},{1,0},{2,3},{3,2},{4,5},{5,4},{6,7},{7,6},{8,9},{9,8},{10,11... | collective-permute-start | bytes 4718600 | tf_op jit(solution)/shard_map/ppermute | solution.py:139
  348.9 8.5 %slice-start.4 = ((s8[5242880]{0:T(1024)(128)(4,1)}), s8[1048576]{0:T(1024)(128)(4,1)S(1)}, s32[]{:S(2)}) async-start(s8[5242880]{0:T(1024)(128)(4,1)} %bitcast.227), calls=%async_computation.10 | async-start | bytes 2097152
  349.9 7.5 %copy-start.40 = (bf16[1280,768]{1,0:T(8,128)(2,1)S(1)}, bf16[1280,768]{1,0:T(8,128)(2,1)}, u32[]{:S(2)}) copy-start(bf16[1280,768]{1,0:T(8,128)(2,1)} %pad_maximum_fusion.5) | copy-start | bytes 5898244
  349.9 7.5 %slice-start.5 = ((s8[5242880]{0:T(1024)(128)(4,1)}), s8[4194304]{0:T(1024)(128)(4,1)S(1)}, s32[]{:S(2)}) async-start(s8[5242880]{0:T(1024)(128)(4,1)} %bitcast.227), calls=%async_computation.11 | async-start | bytes 8388608
  357.3 5.4 %copy-start.41 = (bf16[1280,768]{1,0:T(8,128)(2,1)S(1)}, bf16[1280,768]{1,0:T(8,128)(2,1)}, u32[]{:S(2)}) copy-start(bf16[1280,768]{1,0:T(8,128)(2,1)} %pad_maximum_fusion.6) | copy-start | bytes 5898244
  (60 other events, 167.0 us)

commit v5 on v4

--- a/solution.py
+++ b/solution.py
@@ -134,7 +134,7 @@
         return tuple(p.astype(jnp.bfloat16) for p in (part_gate, part_up, part_down))
 
     sent = weight_parts(other)
-    kept = weight_parts(mine)
+    kept = lax.optimization_barrier(weight_parts(mine))
     swap = [(0, 1), (1, 0)]
     came = tuple(lax.ppermute(p, "replica", swap) for p in sent)
     grad_gate, grad_up, grad_down = (

time: 376 us -> 379 us (level)
  other arithmetic: 43.7 us -> 50.4 us
    broadcast_in_dim x0 -> x3, other arithmetic: none -> 9.65 us  [shards(): (k.astype(jnp.float32) + c.astype(jnp.float32)).astype(jnp.bfloat16)[None]]
    unnamed x170 -> x164, local copies, waits for them, and re-layouts: 45.6 us -> 44.9 us
  transfers between devices with their start and end apart: 9 -> 9, of which waited for: 4 -> 4; matrix products, arithmetic and copies ran while one was open for 53% -> 55% of each run, Pallas kernels for 0% -> 0%
where the time goes in v5:
time: 379 us; the launch traced here: 372 us
  local copies, waits for them, and re-layouts  124 us (33%)
  matrix products  90.3 us (24%)
  starting transfers between devices  63.6 us (17%)
  other arithmetic  50.4 us (13%)
  waiting for transfers between devices  41.4 us (11%)
    all_to_all x6, starting transfers between devices, shards(): lax.all_to_all(jnp.concatenate(pieces, axis=1), 'expert', split_axis=0, c...  62.9 us
    unnamed x164, local copies, waits for them, and re-layouts  44.9 us
    all_to_all x6, waiting for transfers between devices, shards(): lax.all_to_all(jnp.concatenate(pieces, axis=1), 'expert', split_axis=0, c...  41.4 us
    convert_element_type x5, other arithmetic, dequant(): (blocks * scale[:, None, :, None]).reshape(rows, cols).astype(jnp.bfloat16)  17.2 us
    dot_general x4, matrix products, forward_parts(): pre_gate = jnp.dot(xrows, gate_w, preferred_element_type=jnp.float32)  15.5 us
    slice x4, local copies, waits for them, and re-layouts, compute(): row_grad = got[:, span:2 * span].reshape(rows_in, width)  15.1 us
    reshape x4, local copies, waits for them, and re-layouts, compute(): row_grad = got[:, span:2 * span].reshape(rows_in, width)  13.3 us
    reshape x4, local copies, waits for them, and re-layouts, compute(): xrows = got[:, :span].reshape(rows_in, width)  13 us
  transfers between devices with their start and end apart: 9, of which 4 were waited for; matrix products, arithmetic and copies ran while one was open for 55% of the time, Pallas kernels for 0%

profile of v5, /device:TPU:0, one launch (start us, length us, event | category | flops | bytes accessed | tf_op | source)
XLA Modules:
  0.0 372.1 jit_solution(17101685707538662371)
XLA Ops:
  14.1 11.9 %all-to-all-start = ((bf16[64,160,128]{2,1,0:T(8,128)(2,1)}), bf16[64,160,128]{2,1,0:T(8,128)(2,1)}, u32[]{:S(2)}, u32[]{:S(2)}) async-start(bf16[64,160,128]{2,1,0:T(8,128)(2,1)} %pad_maximum_fusion.2), calls=%async_computation | async-start | bytes 5242880 | tf_op jit(solution)/shard_map/all_to_all | solution.py:109
  41.0 4.1 %copy.76 = f32[96,8,16,128]{3,2,1,0:T(8,128)} copy(f32[96,8,16,128]{3,1,2,0:T(8,128)S(1)} %convert_bitcast_fusion.1) | data formatting | bytes 12582912
  45.9 4.0 %copy.72 = f32[96,8,16,128]{3,2,1,0:T(8,128)} copy(f32[96,8,16,128]{3,1,2,0:T(8,128)S(1)} %convert_bitcast_fusion.4) | data formatting | bytes 12582912
  54.9 4.2 %copy.74 = f32[96,8,16,128]{3,2,1,0:T(8,128)} copy(f32[96,8,16,128]{3,1,2,0:T(8,128)S(1)} %convert_bitcast_fusion.3) | data formatting | bytes 12582912
  59.5 5.3 %multiply_convert_fusion = bf16[16,128,6,128]{1,0,3,2:T(8,128)(2,1)} fusion(f32[16,128,6,128]{1,0,3,2:T(8,128)} %bitcast.197, f32[16,6]{0,1:T(8,128)S(1)} %bitcast.231), kind=kLoop, calls=%fused_computation.19 | loop fusion | flops 3145728 | bytes 9437568 | tf_op jit(solution)/shard_map/convert_element_type | solution.py:14
  86.0 11.1 %all-to-all-start.2 = ((bf16[64,160,128]{2,1,0:T(8,128)(2,1)}), bf16[64,160,128]{2,1,0:T(8,128)(2,1)}, u32[]{:S(2)}, u32[]{:S(2)}) async-start(bf16[64,160,128]{2,1,0:T(8,128)(2,1)} %pad_maximum_fusion.3), calls=%async_computation.2 | async-start | bytes 5242880 | tf_op jit(solution)/shard_map/all_to_all | solution.py:109
  126.8 4.8 %all-to-all-done.2 = bf16[64,160,128]{2,1,0:T(8,128)(2,1)} async-done(((bf16[64,160,128]{2,1,0:T(8,128)(2,1)}), bf16[64,160,128]{2,1,0:T(8,128)(2,1)}, u32[]{:S(2)}, u32[]{:S(2)}) %all-to-all-start.2) | async-done | bytes 2621472 | tf_op jit(solution)/shard_map/all_to_all | solution.py:109
  131.6 6.5 %all-to-all-start.1 = ((bf16[64,240,128]{2,1,0:T(8,128)(2,1)}), bf16[64,240,128]{2,1,0:T(8,128)(2,1)}, u32[]{:S(2)}, u32[]{:S(2)}) async-start(bf16[64,240,128]{2,1,0:T(8,128)(2,1)} %pad_maximum_fusion), calls=%async_computation.1 | async-start | bytes 7864320 | tf_op jit(solution)/shard_map/all_to_all | solution.py:109
  177.9 8.8 %all-to-all-done.1 = bf16[64,240,128]{2,1,0:T(8,128)(2,1)} async-done(((bf16[64,240,128]{2,1,0:T(8,128)(2,1)}), bf16[64,240,128]{2,1,0:T(8,128)(2,1)}, u32[]{:S(2)}, u32[]{:S(2)}) %all-to-all-start.1) | async-done | bytes 3932192 | tf_op jit(solution)/shard_map/all_to_all | solution.py:109
  186.8 12.8 %all-to-all-start.3 = ((bf16[64,240,128]{2,1,0:T(8,128)(2,1)}), bf16[64,240,128]{2,1,0:T(8,128)(2,1)}, u32[]{:S(2)}, u32[]{:S(2)}) async-start(bf16[64,240,128]{2,1,0:T(8,128)(2,1)} %pad_maximum_fusion.1), calls=%async_computation.3 | async-start | bytes 7864320 | tf_op jit(solution)/shard_map/all_to_all | solution.py:109
  207.0 4.1 %fusion.113 = (bf16[64,80,128]{2,1,0:T(8,128)(2,1)}, bf16[64,80,128]{2,1,0:T(8,128)(2,1)}, bf16[64,80,128]{2,1,0:T(8,128)(2,1)}) fusion(bf16[64,240,128]{2,1,0:T(8,128)(2,1)} %all-to-all-done.1), kind=kLoop, calls=%fused_computation.221 | loop fusion | bytes 7864320 | tf_op jit(solution)/shard_map/slice | solution.py:90
  229.7 16.3 %all-to-all-done.3 = bf16[64,240,128]{2,1,0:T(8,128)(2,1)} async-done(((bf16[64,240,128]{2,1,0:T(8,128)(2,1)}), bf16[64,240,128]{2,1,0:T(8,128)(2,1)}, u32[]{:S(2)}, u32[]{:S(2)}) %all-to-all-start.3) | async-done | bytes 3932192 | tf_op jit(solution)/shard_map/all_to_all | solution.py:109
  246.0 4.2 %fusion.112 = (bf16[64,80,128]{2,1,0:T(8,128)(2,1)}, bf16[64,80,128]{2,1,0:T(8,128)(2,1)}, bf16[64,80,128]{2,1,0:T(8,128)(2,1)}) fusion(bf16[64,240,128]{2,1,0:T(8,128)(2,1)} %all-to-all-done.3), kind=kLoop, calls=%fused_computation.220 | loop fusion | bytes 7864320 | tf_op jit(solution)/shard_map/slice | solution.py:90
  253.4 4.5 %fusion.7 = f32[320,768]{1,0:T(8,128)} fusion(bf16[320,2048]{1,0:T(8,128)(2,1)} %reshape.510, bf16[96,8,16,128]{3,2,1,0:T(8,128)(2,1)} %bitcast.215), kind=kOutput, calls=%fused_computation.27 | convolution fusion | flops 1006632960 | bytes 5439488 | tf_op jit(solution)/shard_map/dot_general | solution.py:18
  276.1 10.3 %all-to-all-start.4 = ((bf16[64,80,128]{2,1,0:T(8,128)(2,1)}), bf16[64,80,128]{2,1,0:T(8,128)(2,1)S(1)}, u32[]{:S(2)}, u32[]{:S(2)}) async-start(bf16[64,80,128]{2,1,0:T(8,128)(2,1)} %reshape.507), calls=%async_computation.4 | async-start | bytes 2621440 | tf_op jit(solution)/shard_map/all_to_all | solution.py:109
  286.4 4.9 %fusion.34 = bf16[320,2048]{1,0:T(8,128)(2,1)} fusion(f32[320,2048]{1,0:T(8,128)} %fusion.120, bf16[320,768]{1,0:T(8,128)(2,1)S(1)} %copy-done.57, bf16[2048,768]{0,1:T(8,128)(2,1)} %fusion.1), kind=kOutput, calls=%fused_computation.67 | convolution fusion | flops 1007943680 | bytes 7569408 | tf_op jit(solution)/shard_map/dot_general | solution.py:95
  297.8 6.7 %convolution_convert_fusion.2 = bf16[2048,384]{1,0:T(8,128)(2,1)} fusion(bf16[1280,2048]{1,0:T(8,128)(2,1)} %constant_dynamic-update-slice_fusion, bf16[1280,768]{1,0:T(8,128)(2,1)S(1)} %copy-done.38, s32[]{:T(128)S(6)} %select_n.159), kind=kOutput, calls=%fused_computation.60 | convolution fusion | flops 2014052352 | bytes 7798788 | tf_op jit(solution)/shard_map/dot_general | solution.py:131
  304.5 4.2 %convolution_convert_fusion.5 = bf16[2048,384]{1,0:T(8,128)(2,1)} fusion(bf16[1280,2048]{1,0:T(8,128)(2,1)S(1)} %copy-done.61, bf16[1280,768]{1,0:T(8,128)(2,1)S(1)} %copy-done.38, s32[]{:T(128)S(6)} %select_n.158), kind=kOutput, calls=%fused_computation.63 | convolution fusion | flops 2014052352 | bytes 7798788 | tf_op jit(solution)/shard_map/dot_general | solution.py:131
  311.9 6.6 %convolution_convert_fusion.3 = bf16[384,2048]{1,0:T(8,128)(2,1)} fusion(bf16[1280,2048]{1,0:T(8,128)(2,1)} %constant_dynamic-update-slice_fusion.4, bf16[1280,768]{1,0:T(8,128)(2,1)S(1)} %pad_maximum_fusion.6, s32[]{:T(128)S(6)} %select_n.158), kind=kOutput, calls=%fused_computation.61 | convolution fusion | flops 2014052352 | bytes 7798788 | tf_op jit(solution)/shard_map/dot_general | solution.py:133
  318.7 4.0 %convolution_convert_fusion.4 = bf16[2048,384]{1,0:T(8,128)(2,1)} fusion(bf16[1280,2048]{1,0:T(8,128)(2,1)S(1)} %copy-done.61, bf16[1280,768]{1,0:T(8,128)(2,1)S(1)} %pad_maximum_fusion.5, s32[]{:T(128)S(6)} %select_n.158), kind=kOutput, calls=%fused_computation.62 | convolution fusion | flops 2014052352 | bytes 7798788 | tf_op jit(solution)/shard_map/dot_general | solution.py:132
  322.7 4.0 %convolution_convert_fusion.1 = bf16[2048,384]{1,0:T(8,128)(2,1)} fusion(bf16[1280,2048]{1,0:T(8,128)(2,1)S(1)} %copy-done.61, bf16[1280,768]{1,0:T(8,128)(2,1)S(1)} %pad_maximum_fusion.5, s32[]{:T(128)S(6)} %select_n.159), kind=kOutput, calls=%fused_computation.59 | convolution fusion | flops 2014052352 | bytes 7798788 | tf_op jit(solution)/shard_map/dot_general | solution.py:132
  327.2 10.3 %all-to-all-start.5 = ((bf16[64,80,128]{2,1,0:T(8,128)(2,1)}), bf16[64,80,128]{2,1,0:T(8,128)(2,1)S(1)}, u32[]{:S(2)}, u32[]{:S(2)}) async-start(bf16[64,80,128]{2,1,0:T(8,128)(2,1)} %reshape.511), calls=%async_computation.5 | async-start | bytes 2621440 | tf_op jit(solution)/shard_map/all_to_all | solution.py:109
  337.6 6.3 %convolution_convert_fusion = bf16[384,2048]{1,0:T(8,128)(2,1)} fusion(bf16[1280,2048]{1,0:T(8,128)(2,1)} %constant_dynamic-update-slice_fusion.4, bf16[1280,768]{1,0:T(8,128)(2,1)} %copy-done.37, s32[]{:T(128)S(6)} %select_n.159), kind=kOutput, calls=%fused_computation.58 | convolution fusion | flops 2014052352 | bytes 7798788 | tf_op jit(solution)/shard_map/dot_general | solution.py:133
  347.7 11.5 %all-to-all-done.5 = bf16[64,80,128]{2,1,0:T(8,128)(2,1)S(1)} async-done(((bf16[64,80,128]{2,1,0:T(8,128)(2,1)}), bf16[64,80,128]{2,1,0:T(8,128)(2,1)S(1)}, u32[]{:S(2)}, u32[]{:S(2)}) %all-to-all-start.5) | async-done | bytes 1310752 | tf_op jit(solution)/shard_map/all_to_all | solution.py:109
  (294 shorter events, 198.7 us)
Async XLA Ops:
  5.6 25.6 %copy-start = (bf16[129,16,128]{2,1,0:T(8,128)(2,1)}, bf16[129,16,128]{2,1,0:T(8,128)(2,1)S(1)}, u32[]{:S(2)}) copy-start(bf16[129,16,128]{2,1,0:T(8,128)(2,1)S(1)} %concatenate.34) | copy-start | bytes 1585156
  6.1 27.6 %copy-start.1 = (bf16[129,16,128]{2,1,0:T(8,128)(2,1)}, bf16[129,16,128]{2,1,0:T(8,128)(2,1)S(1)}, u32[]{:S(2)}) copy-start(bf16[129,16,128]{2,1,0:T(8,128)(2,1)S(1)} %concatenate.33) | copy-start | bytes 1585156
  14.1 72.0 %all-to-all-start = ((bf16[64,160,128]{2,1,0:T(8,128)(2,1)}), bf16[64,160,128]{2,1,0:T(8,128)(2,1)}, u32[]{:S(2)}, u32[]{:S(2)}) async-start(bf16[64,160,128]{2,1,0:T(8,128)(2,1)} %pad_maximum_fusion.2), calls=%async_computation | async-start | bytes 5242880 | tf_op jit(solution)/shard_map/all_to_all | solution.py:109
  59.5 5.3 %copy-start.21 = (bf16[320,16,128]{2,1,0:T(8,128)(2,1)S(1)}, bf16[320,16,128]{2,1,0:T(8,128)(2,1)}, u32[]{:S(2)}) copy-start(bf16[320,16,128]{2,1,0:T(8,128)(2,1)} %gather_fusion.1) | copy-start | bytes 3932164
  59.5 9.9 %slice-start = ((s8[6291456]{0:T(1024)(128)(4,1)}), s8[4194304]{0:T(1024)(128)(4,1)S(1)}, s32[]{:S(2)}) async-start(s8[6291456]{0:T(1024)(128)(4,1)} %bitcast.191), calls=%async_computation.6 | async-start | bytes 8388608
  64.8 4.6 %slice-start.1 = ((s8[6291456]{0:T(1024)(128)(4,1)}), s8[2097152]{0:T(1024)(128)(4,1)S(1)}, s32[]{:S(2)}) async-start(s8[6291456]{0:T(1024)(128)(4,1)} %bitcast.191), calls=%async_computation.7 | async-start | bytes 4194304
  86.0 45.6 %all-to-all-start.2 = ((bf16[64,160,128]{2,1,0:T(8,128)(2,1)}), bf16[64,160,128]{2,1,0:T(8,128)(2,1)}, u32[]{:S(2)}, u32[]{:S(2)}) async-start(bf16[64,160,128]{2,1,0:T(8,128)(2,1)} %pad_maximum_fusion.3), calls=%async_computation.2 | async-start | bytes 5242880 | tf_op jit(solution)/shard_map/all_to_all | solution.py:109
  131.6 55.2 %all-to-all-start.1 = ((bf16[64,240,128]{2,1,0:T(8,128)(2,1)}), bf16[64,240,128]{2,1,0:T(8,128)(2,1)}, u32[]{:S(2)}, u32[]{:S(2)}) async-start(bf16[64,240,128]{2,1,0:T(8,128)(2,1)} %pad_maximum_fusion), calls=%async_computation.1 | async-start | bytes 7864320 | tf_op jit(solution)/shard_map/all_to_all | solution.py:109
  138.1 6.3 %copy-start.62 = (s32[128,8]{0,1:T(8,128)S(1)}, s32[128,8]{0,1:T(8,128)}, u32[]{:S(2)}) copy-start(s32[128,8]{0,1:T(8,128)} %param.14) | copy-start | bytes 12292
  186.8 59.2 %all-to-all-start.3 = ((bf16[64,240,128]{2,1,0:T(8,128)(2,1)}), bf16[64,240,128]{2,1,0:T(8,128)(2,1)}, u32[]{:S(2)}, u32[]{:S(2)}) async-start(bf16[64,240,128]{2,1,0:T(8,128)(2,1)} %pad_maximum_fusion.1), calls=%async_computation.3 | async-start | bytes 7864320 | tf_op jit(solution)/shard_map/all_to_all | solution.py:109
  274.6 11.8 %copy-start.57 = (bf16[320,768]{1,0:T(8,128)(2,1)S(1)}, bf16[320,768]{1,0:T(8,128)(2,1)}, u32[]{:S(2)}) copy-start(bf16[320,768]{1,0:T(8,128)(2,1)} %get-tuple-element.48) | copy-start | bytes 1474564
  276.1 51.1 %all-to-all-start.4 = ((bf16[64,80,128]{2,1,0:T(8,128)(2,1)}), bf16[64,80,128]{2,1,0:T(8,128)(2,1)S(1)}, u32[]{:S(2)}, u32[]{:S(2)}) async-start(bf16[64,80,128]{2,1,0:T(8,128)(2,1)} %reshape.507), calls=%async_computation.4 | async-start | bytes 2621440 | tf_op jit(solution)/shard_map/all_to_all | solution.py:109
  297.8 6.7 %copy-start.61 = (bf16[1280,2048]{1,0:T(8,128)(2,1)S(1)}, bf16[1280,2048]{1,0:T(8,128)(2,1)}, u32[]{:S(2)}) copy-start(bf16[1280,2048]{1,0:T(8,128)(2,1)} %constant_dynamic-update-slice_fusion) | copy-start | bytes 15728644
  304.5 4.2 %copy-start.10 = (bf16[320,2048]{1,0:T(8,128)(2,1)S(1)}, bf16[320,2048]{1,0:T(8,128)(2,1)}, u32[]{:S(2)}) copy-start(bf16[320,2048]{1,0:T(8,128)(2,1)} %reshape.505) | copy-start | bytes 3932164
  304.5 57.8 %collective-permute-start = (bf16[2048,384]{1,0:T(8,128)(2,1)}, bf16[2048,384]{1,0:T(8,128)(2,1)}, u32[]{:S(2)}, u32[]{:S(2)}) collective-permute-start(bf16[2048,384]{1,0:T(8,128)(2,1)} %convolution_convert_fusion.2), channel_id=1, source_target_pairs={{0,1},{1,0},{2,3},{3,2},{4,5},{5,4},{6,7},{7,6},{8,9},{9,8},{10,11... | collective-permute-start | bytes 4718600 | tf_op jit(solution)/shard_map/ppermute | solution.py:139
  311.9 6.7 %copy-start.37 = (bf16[1280,768]{1,0:T(8,128)(2,1)}, bf16[1280,768]{1,0:T(8,128)(2,1)S(1)}, u32[]{:S(2)}) copy-start(bf16[1280,768]{1,0:T(8,128)(2,1)S(1)} %pad_maximum_fusion.6) | copy-start | bytes 5898244
  311.9 6.7 %copy-start.50 = (bf16[320,768]{1,0:T(8,128)(2,1)S(1)}, bf16[320,768]{1,0:T(8,128)(2,1)}, u32[]{:S(2)}) copy-start(bf16[320,768]{1,0:T(8,128)(2,1)} %copy-done.49) | copy-start | bytes 1474564
  311.9 6.6 %copy-start.53 = (bf16[320,768]{1,0:T(8,128)(2,1)S(1)}, bf16[320,768]{1,0:T(8,128)(2,1)}, u32[]{:S(2)}) copy-start(bf16[320,768]{1,0:T(8,128)(2,1)} %copy-done.52) | copy-start | bytes 1474564
  311.9 6.6 %copy-start.58 = (bf16[320,768]{1,0:T(8,128)(2,1)S(1)}, bf16[320,768]{1,0:T(8,128)(2,1)}, u32[]{:S(2)}) copy-start(bf16[320,768]{1,0:T(8,128)(2,1)} %get-tuple-element.48) | copy-start | bytes 1474564
  326.7 38.9 %collective-permute-start.1 = (bf16[2048,384]{1,0:T(8,128)(2,1)}, bf16[2048,384]{1,0:T(8,128)(2,1)}, u32[]{:S(2)}, u32[]{:S(2)}) collective-permute-start(bf16[2048,384]{1,0:T(8,128)(2,1)} %convolution_convert_fusion.1), channel_id=1, source_target_pairs={{0,1},{1,0},{2,3},{3,2},{4,5},{5,4},{6,7},{7,6},{8,9},{9,8},{10,11... | collective-permute-start | bytes 4718600 | tf_op jit(solution)/shard_map/ppermute | solution.py:139
  327.2 32.0 %all-to-all-start.5 = ((bf16[64,80,128]{2,1,0:T(8,128)(2,1)}), bf16[64,80,128]{2,1,0:T(8,128)(2,1)S(1)}, u32[]{:S(2)}, u32[]{:S(2)}) async-start(bf16[64,80,128]{2,1,0:T(8,128)(2,1)} %reshape.511), calls=%async_computation.5 | async-start | bytes 2621440 | tf_op jit(solution)/shard_map/all_to_all | solution.py:109
  337.6 6.5 %copy-start.23 = (bf16[64,80,128]{2,1,0:T(8,128)(2,1)S(1)}, bf16[64,80,128]{2,1,0:T(8,128)(2,1)}, u32[]{:S(2)}) copy-start(bf16[64,80,128]{2,1,0:T(8,128)(2,1)} %get-tuple-element.32) | copy-start | bytes 3932164
  343.9 24.8 %collective-permute-start.2 = (bf16[384,2048]{1,0:T(8,128)(2,1)}, bf16[384,2048]{1,0:T(8,128)(2,1)}, u32[]{:S(2)}, u32[]{:S(2)}) collective-permute-start(bf16[384,2048]{1,0:T(8,128)(2,1)} %convolution_convert_fusion), channel_id=1, source_target_pairs={{0,1},{1,0},{2,3},{3,2},{4,5},{5,4},{6,7},{7,6},{8,9},{9,8},{10,11... | collective-permute-start | bytes 4718600 | tf_op jit(solution)/shard_map/ppermute | solution.py:139
  361.2 4.5 %copy-start.46 = (bf16[2048,384]{1,0:T(8,128)(2,1)S(1)}, bf16[2048,384]{1,0:T(8,128)(2,1)}, u32[]{:S(2)}) copy-start(bf16[2048,384]{1,0:T(8,128)(2,1)} %convolution_convert_fusion.4) | copy-start | bytes 4718596
  (57 other events, 153.3 us)
